TPU v7x, 32 devices: a whole 2x2x4 slice. The times are simulated.
32 devices in a mesh: gy: 16 (over z, y, core), gz: 2 (over x).
Axes of the slice: x: 2, y: 2, z: 4, core: 2. Of those that a mesh axis runs over, the one named last changes fastest.
Arguments:
- mag_start: float32 [2, 256, 256, 256], P(None, 'gy', 'gz'), may hold values from -3 to 3
- mag_middle: float32 [2, 256, 256, 256], P(None, 'gy', 'gz'), may hold values from -3 to 3
- adjoint_end: float32 [2, 256, 256, 256], P(None, 'gy', 'gz'), may hold values from -3 to 3
- phase: float32 [256, 256, 256], P('gy', 'gz'), may hold values from -4 to 4
- labels: int32 [256, 256, 256], P('gy', 'gz'), may hold values from 0 to 3
Outputs:
- adjoint_start: float32 [2, 256, 256, 256], P(None, 'gy', 'gz')
- chi_grad: float32 [256, 256, 256], P('gy', 'gz')
All inputs are finite; a program needn't handle non-finite values.
Results may differ from a plain program's by a relative error of at most 0.0003.
Values sent between devices are 32-bit elements; how exact they have to be, the bound alone decides.
No kernel may reach another device: no remote copies, remote signals or barrier semaphores. Data moves between devices by JAX's collectives and lax.ppermute only.
A program may use at most 192 MiB of HBM per device.

v0:
```python
import functools
import math

import jax
import jax.numpy as jnp
from jax import lax
from jax.experimental import pallas as pl
from jax.experimental.pallas import tpu as pltpu
from jax.sharding import PartitionSpec as P


def signed_freq(index, length):
    return jnp.where(index < length // 2, index, index - length)


def dipole_block(freq_y, freq_z, freq_x):
    square_z = freq_z * freq_z
    total = freq_y * freq_y + square_z + freq_x * freq_x
    ratio = square_z.astype(jnp.float32) / jnp.maximum(total, 1).astype(jnp.float32)
    return jnp.where(total == 0, jnp.float32(0.0), jnp.float32(1.0 / 3.0) - ratio)


def cas_table(length):
    index = jnp.arange(length, dtype=jnp.int32)
    product = index[:, None] * index[None, :] % length
    angle = product.astype(jnp.float32) * (2.0 * math.pi / length)
    return jnp.cos(angle) + jnp.sin(angle)


def along(spec, table, values):
    return jnp.einsum(spec, table, values, precision=lax.Precision.HIGH)


def plane_update(centre, below, above, z_low, z_high):
    length_z, length_x = centre.shape
    row = lax.broadcasted_iota(jnp.int32, centre.shape, 0)
    up = jnp.where(row == 0, z_low, pltpu.roll(centre, 1, 0))
    down = jnp.where(row == length_z - 1, z_high, pltpu.roll(centre, length_z - 1, 0))
    total = below + above + up + down
    total = total + pltpu.roll(centre, 1, 1) + pltpu.roll(centre, length_x - 1, 1)
    return centre + 0.15 * (total - 6.0 * centre)


def neighbour_planes(cur_ref, prev_ref, next_ref, y_low_ref, y_high_ref, rows, field, comp, r):
    step = pl.program_id(0)
    last = pl.num_programs(0) - 1
    if r == 0:
        below = jnp.where(step == 0, y_low_ref[field], prev_ref[comp, 0])
    else:
        below = cur_ref[comp, r - 1]
    if r == rows - 1:
        above = jnp.where(step == last, y_high_ref[field], next_ref[comp, 0])
    else:
        above = cur_ref[comp, r + 1]
    return below, above


def write_edges(step, rows, r, values, y_first_ref, y_last_ref, z_first_ref, z_last_ref):
    for c, value in enumerate(values):
        z_first_ref[c, r] = value[0:1]
        z_last_ref[c, r] = value[value.shape[0] - 1:]
    if r == 0:
        @pl.when(step == 0)
        def _():
            for c, value in enumerate(values):
                y_first_ref[c] = value
    if r == rows - 1:
        @pl.when(step == pl.num_programs(0) - 1)
        def _():
            for c, value in enumerate(values):
                y_last_ref[c] = value


def factor_kernel(lam_ref, phase_ref, labels_ref, factor_ref, w_ref, *edge_refs, rows):
    step = pl.program_id(0)
    for r in range(rows):
        labels = labels_ref[r]
        rate = jnp.where(labels == 1, 0.3, 0.02)
        rate = jnp.where(labels == 2, 0.6, rate)
        rate = jnp.where(labels == 3, 1.2, rate).astype(jnp.float32)
        decay = jnp.exp(-rate)
        phase = phase_ref[r]
        f_real = decay * jnp.cos(phase)
        f_imag = decay * jnp.sin(phase)
        lam_real = lam_ref[0, r]
        lam_imag = lam_ref[1, r]
        w_real = f_real * lam_real - f_imag * lam_imag
        w_imag = f_real * lam_imag + f_imag * lam_real
        factor_ref[0, r] = f_real
        factor_ref[1, r] = f_imag
        w_ref[0, r] = w_real
        w_ref[1, r] = w_imag
        write_edges(step, rows, r, [w_real, w_imag], *edge_refs)


def edge_outputs(comps, length_y, length_z, length_x, rows):
    plane = jax.ShapeDtypeStruct((comps, length_z, length_x), jnp.float32)
    row = jax.ShapeDtypeStruct((comps, length_y, 1, length_x), jnp.float32)
    plane_spec = pl.BlockSpec((comps, length_z, length_x), lambda i: (0, 0, 0))
    row_spec = pl.BlockSpec((comps, rows, 1, length_x), lambda i: (0, i, 0, 0))
    return [plane, plane, row, row], [plane_spec, plane_spec, row_spec, row_spec]


def first_kernel(*refs, rows):
    (mm_ref, mm_prev, mm_next, ms_ref, ms_prev, ms_next, w_ref, w_prev, w_next,
     factor_ref, y_low_ref, y_high_ref, z_low_ref, z_high_ref, pg_ref, w2_ref) = refs[:16]
    step = pl.program_id(0)
    fields = ((mm_ref, mm_prev, mm_next), (ms_ref, ms_prev, ms_next), (w_ref, w_prev, w_next))
    for r in range(rows):
        new = []
        for f, (cur, prev, nxt) in enumerate(fields):
            pair = []
            for comp in range(2):
                below, above = neighbour_planes(cur, prev, nxt, y_low_ref, y_high_ref, rows, 2 * f + comp, comp, r)
                pair.append(plane_update(cur[comp, r], below, above,
                                         z_low_ref[2 * f + comp, r], z_high_ref[2 * f + comp, r]))
            new.append(pair)
        (u1_real, u1_imag), (u2_real, u2_imag), (lam_real, lam_imag) = new
        w_real = w_ref[0, r]
        w_imag = w_ref[1, r]
        f_real = factor_ref[0, r]
        f_imag = factor_ref[1, r]
        w2_real = f_real * lam_real - f_imag * lam_imag
        w2_imag = f_real * lam_imag + f_imag * lam_real
        grad = w_real * u1_imag - w_imag * u1_real
        pg_ref[r] = grad + (w2_real * u2_imag - w2_imag * u2_real)
        w2_ref[0, r] = w2_real
        w2_ref[1, r] = w2_imag
        write_edges(step, rows, r, [w2_real, w2_imag], *refs[16:])


def second_kernel(w_ref, w_prev, w_next, y_low_ref, y_high_ref, z_low_ref, z_high_ref, out_ref, *, rows):
    for r in range(rows):
        for comp in range(2):
            below, above = neighbour_planes(w_ref, w_prev, w_next, y_low_ref, y_high_ref, rows, comp, comp, r)
            out_ref[comp, r] = plane_update(w_ref[comp, r], below, above,
                                            z_low_ref[comp, r], z_high_ref[comp, r])


def block_rows(length_y):
    rows = 4
    while length_y % rows:
        rows //= 2
    return rows


def field_specs(shape, rows):
    comps, length_y, length_z, length_x = shape
    cur = pl.BlockSpec((comps, rows, length_z, length_x), lambda i: (0, i, 0, 0))
    prev = pl.BlockSpec((comps, 1, length_z, length_x),
                        lambda i: (0, jnp.maximum(i * rows - 1, 0), 0, 0))
    nxt = pl.BlockSpec((comps, 1, length_z, length_x),
                       lambda i: (0, jnp.minimum(i * rows + rows, length_y - 1), 0, 0))
    return [cur, prev, nxt]


def send_edges(y_first, y_last, z_first, z_last):
    results = []
    for axis, first, last in (("gy", y_first, y_last), ("gz", z_first, z_last)):
        count = lax.axis_size(axis)
        up = [(i, (i + 1) % count) for i in range(count)]
        down = [(j, i) for i, j in up]
        results.extend([lax.ppermute(last, axis, up), lax.ppermute(first, axis, down)])
    return results


def input_edges(fields):
    y_first = jnp.concatenate([f[:, 0] for f in fields])
    y_last = jnp.concatenate([f[:, -1] for f in fields])
    z_first = jnp.concatenate([f[:, :, 0:1] for f in fields])
    z_last = jnp.concatenate([f[:, :, -1:] for f in fields])
    return [y_first, y_last, z_first, z_last]


def backward_sections(mag_start, mag_middle, adjoint_end, phase, labels):
    _, length_y, length_z, length_x = mag_start.shape
    rows = block_rows(length_y)
    grid = (length_y // rows,)
    plane = jax.ShapeDtypeStruct((length_y, length_z, length_x), jnp.float32)
    pair = jax.ShapeDtypeStruct((2, length_y, length_z, length_x), jnp.float32)
    cur = pl.BlockSpec((2, rows, length_z, length_x), lambda i: (0, i, 0, 0))
    cur_plane = pl.BlockSpec((rows, length_z, length_x), lambda i: (i, 0, 0))
    whole = lambda shape: pl.BlockSpec(shape, lambda i: (0,) * len(shape))
    zspec = lambda comps: pl.BlockSpec((comps, rows, 1, length_x), lambda i: (0, i, 0, 0))
    edge_shapes, edge_specs = edge_outputs(2, length_y, length_z, length_x, rows)
    factor, w_first, *w_edges = pl.pallas_call(
        functools.partial(factor_kernel, rows=rows),
        grid=grid,
        in_specs=[cur, cur_plane, cur_plane],
        out_specs=[cur, cur] + edge_specs,
        out_shape=[pair, pair] + edge_shapes,
    )(adjoint_end, phase, labels)
    mag_edges = input_edges([mag_middle, mag_start])
    halos = send_edges(*[jnp.concatenate([a, b]) for a, b in zip(mag_edges, w_edges)])
    phase_grad, w_second, *w2_edges = pl.pallas_call(
        functools.partial(first_kernel, rows=rows),
        grid=grid,
        in_specs=field_specs(mag_middle.shape, rows) + field_specs(mag_start.shape, rows)
        + field_specs(w_first.shape, rows)
        + [cur, whole((6, length_z, length_x)), whole((6, length_z, length_x)), zspec(6), zspec(6)],
        out_specs=[cur_plane, cur] + edge_specs,
        out_shape=[plane, pair] + edge_shapes,
    )(mag_middle, mag_middle, mag_middle, mag_start, mag_start, mag_start,
      w_first, w_first, w_first, factor, *halos)
    halos = send_edges(*w2_edges)
    lam = pl.pallas_call(
        functools.partial(second_kernel, rows=rows),
        grid=grid,
        in_specs=field_specs(w_second.shape, rows)
        + [whole((2, length_z, length_x)), whole((2, length_z, length_x)), zspec(2), zspec(2)],
        out_specs=cur,
        out_shape=pair,
    )(w_second, w_second, w_second, *halos)
    return (lam, phase_grad)


def dipole_adjoint(phase_grad):
    count_y = lax.axis_size("gy")
    count_z = lax.axis_size("gz")
    parts = count_y * count_z
    block_y, block_z, length_x = phase_grad.shape
    length_y = block_y * count_y
    length_z = block_z * count_z
    block_x = length_x // parts
    table_x = cas_table(length_x)
    table_y = cas_table(length_y)
    table_z = cas_table(length_z)
    scale = 1.0 / (float(length_y) * float(length_z) * float(length_x))
    spec = along("kn,yzn->kyz", table_x, phase_grad)
    spec = spec.reshape(parts, block_x, block_y, block_z)
    spec = lax.all_to_all(spec, ("gy", "gz"), 0, 0, tiled=True)
    spec = spec.reshape(count_y, count_z, block_x, block_y, block_z)
    spec = spec.transpose(2, 0, 3, 1, 4).reshape(block_x, length_y, length_z)
    spec = along("kz,xyz->xyk", table_z, spec)
    spec = along("ky,xyz->xkz", table_y, spec)
    freq_y = signed_freq(jnp.arange(length_y, dtype=jnp.int32), length_y)
    freq_z = signed_freq(jnp.arange(length_z, dtype=jnp.int32), length_z)
    index = lax.axis_index("gy") * count_z + lax.axis_index("gz")
    freq_x = signed_freq(index * block_x + jnp.arange(block_x, dtype=jnp.int32), length_x)
    kernel = dipole_block(freq_y[None, :, None], freq_z[None, None, :], freq_x[:, None, None])
    spec = spec * kernel
    spec = along("ky,xyz->xkz", table_y, spec)
    spec = along("kz,xyz->xyk", table_z, spec)
    spec = spec.reshape(block_x, count_y, block_y, count_z, block_z)
    spec = spec.transpose(1, 3, 0, 2, 4).reshape(parts, block_x, block_y, block_z)
    spec = lax.all_to_all(spec, ("gy", "gz"), 0, 0, tiled=True)
    spec = spec.reshape(length_x, block_y, block_z)
    return along("kn,nyz->yzk", table_x, spec) * scale


def per_device(mag_start, mag_middle, adjoint_end, phase, labels):
    lam, phase_grad = backward_sections(mag_start, mag_middle, adjoint_end, phase, labels)
    chi_grad = dipole_adjoint(phase_grad)
    return (lam, chi_grad)


def solution(mesh):
    return jax.shard_map(
        per_device,
        mesh=mesh,
        in_specs=(
            P(None, "gy", "gz", None),
            P(None, "gy", "gz", None),
            P(None, "gy", "gz", None),
            P("gy", "gz", None),
            P("gy", "gz", None),
        ),
        out_specs=(P(None, "gy", "gz", None), P("gy", "gz", None)),
        check_vma=False,
    )
```

profile of v0, /device:TPU:16, one launch (start us, length us, event | category | flops | bytes accessed | tf_op | source)
XLA Modules:
  0.0 199.3 jit_solution(11162405033507926297)
XLA Ops:
  0.6 1.3 slice_bitcast_fusion
  1.9 12.2 %shard_map.68 = (f32[2,16,128,256]{3,2,1,0:T(8,128)}, f32[2,16,128,256]{3,2,1,0:T(8,128)}, f32[2,128,256]{2,1,0:T(8,128)}, f32[2,128,256]{2,1,0:T(8,128)}, f32[2...) custom-call(f32[2,16,128,256]{3,2,1,0:T(8,128)} %lam_ref.1, f32[16,128,256]{2,1,0:T(8,128)} %phase_ref.1, ...), custom_call_target="tpu_custom_call" | custom-call | tf_op jit(solution)/shard_map/pallas_call | solution.py:186
  14.1 0.0 copy-start.9
  14.1 1.0 pad_maximum_fusion.1
  15.1 0.9 collective-permute-start.1
  16.0 1.0 pad_maximum_fusion
  17.0 0.1 collective-permute-start
  17.1 1.3 fusion.65
  18.4 0.1 pad_maximum_fusion.2
  18.5 1.6 collective-permute-start.2
  20.1 0.1 pad_maximum_fusion.3
  20.2 0.6 collective-permute-start.3
  20.8 3.5 %collective-permute-done.2.refs_12_ = f32[6,16,1,256]{3,2,1,0:T(1,128)S(1)} collective-permute-done((f32[6,16,1,256]{3,2,1,0:T(1,128)S(1)}, f32[6,16,1,256]{3,2,1,0:T(1,128)S(1)}, u32[]{:S(2)}, u32[]{:S(2)}) %collective-permute-start.2) | collective-permute-done | bytes 98336 | tf_op jit(solution)/shard_map/ppermute | solution.py:163
  24.2 1.9 collective-permute-done.3.refs_13_
  26.2 0.0 collective-permute-done.1.refs_11_
  26.2 3.3 %collective-permute-done.refs_10_ = f32[6,128,256]{2,1,0:T(8,128)S(1)} collective-permute-done((f32[6,128,256]{2,1,0:T(8,128)S(1)}, f32[6,128,256]{2,1,0:T(8,128)S(1)}, u32[]{:S(2)}, u32[]{:S(2)}) %collective-permute-start) | collective-permute-done | bytes 786464 | tf_op jit(solution)/shard_map/ppermute | solution.py:163
  29.5 0.0 copy-done
  29.5 1.0 copy-done.1
  30.5 14.8 %shard_map.69 = (f32[16,128,256]{2,1,0:T(8,128)}, f32[2,16,128,256]{3,2,1,0:T(8,128)}, f32[2,128,256]{2,1,0:T(8,128)}, f32[2,128,256]{2,1,0:T(8,128)}, f32[2,16,...) custom-call(f32[2,16,128,256]{3,2,1,0:T(8,128)} %refs_2_.1, f32[2,16,128,256]{3,2,1,0:T(8,128)} %refs_2_.1, ...), custom_call_target="tpu_custom_call" | custom-call | tf_op jit(solution)/shard_map/pallas_call | solution.py:195
  45.3 3.7 %convolution_bitcast_fusion = f32[32,8,16,128]{3,1,0,2:T(8,128)S(1)} fusion(f32[16,128,256]{2,1,0:T(8,128)} %get-tuple-element.25), kind=kOutput, calls=%fused_computation.13 | convolution fusion | flops 806289408 | bytes 4194304 | tf_op jit(solution)/shard_map/kn,yzn->kyz/dot_general | solution.py:31
  49.0 2.5 %copy.21 = f32[32,8,16,128]{3,2,1,0:T(8,128)} copy(f32[32,8,16,128]{3,1,0,2:T(8,128)S(1)} %convolution_bitcast_fusion) | data formatting | bytes 4194304 | tf_op jit(solution)/shard_map/reshape | solution.py:230
  51.5 12.5 %all-to-all-start = ((f32[32,8,16,128]{3,2,1,0:T(8,128)}), f32[32,8,16,128]{3,2,1,0:T(8,128)S(1)}, u32[]{:S(2)}, u32[]{:S(2)}) async-start(f32[32,8,16,128]{3,2,1,0:T(8,128)} %copy.21), calls=%async_computation | async-start | bytes 4194304 | tf_op jit(solution)/shard_map/all_to_all | solution.py:231
  64.1 0.1 broadcast_add_fusion
  64.2 47.0 %all-to-all-done = f32[32,8,16,128]{3,2,1,0:T(8,128)S(1)} async-done(((f32[32,8,16,128]{3,2,1,0:T(8,128)}), f32[32,8,16,128]{3,2,1,0:T(8,128)S(1)}, u32[]{:S(2)}, u32[]{:S(2)}) %all-to-all-start) | async-done | bytes 2097184 | tf_op jit(solution)/shard_map/all_to_all | solution.py:231
  111.1 2.9 %copy.22 = f32[8,16,16,2,128]{4,3,2,1,0:T(2,128)} copy(f32[8,16,16,2,128]{4,2,0,3,1:T(8,128)S(1)} %bitcast.49) | data formatting | bytes 4194304 | tf_op jit(solution)/shard_map/transpose | solution.py:233
  114.1 2.9 %reshape.89 = f32[8,256,256]{2,1,0:T(8,128)S(1)} reshape(f32[8,16,16,2,128]{4,3,2,1,0:T(2,128)} %copy.22) | data formatting | bytes 4194304 | tf_op jit(solution)/shard_map/reshape | solution.py:233
  117.0 2.1 %fusion.29 = f32[8,256,256]{1,2,0:T(8,128)S(1)} fusion(f32[8,256,256]{2,1,0:T(8,128)S(1)} %reshape.89), kind=kOutput, calls=%fused_computation.34 | convolution fusion | flops 806289408 | bytes 4194304 | tf_op jit(solution)/shard_map/kz,xyz->xyk/dot_general | solution.py:31
  119.1 2.1 %fusion.27 = f32[8,256,256]{2,1,0:T(8,128)S(1)} fusion(f32[8,256,256]{1,2,0:T(8,128)S(1)} %fusion.29), kind=kOutput, calls=%fused_computation.32 | convolution fusion | flops 806289408 | bytes 4194304 | tf_op jit(solution)/shard_map/ky,xyz->xkz/dot_general | solution.py:31
  121.2 2.6 %fusion.9 = f32[8,256,256]{2,1,0:T(8,128)S(1)} fusion(f32[8,256,256]{2,1,0:T(8,128)S(1)} %fusion.27, f32[256]{0:T(256)S(1)} %fusion.37, s32[8]{0:T(128)S(1)} %fusion.36, s32[256,256]{0,1:T(8,128)S(1)} %broadcast_add_fusion), kind=kOutput, calls=%fused_computation.11 | convolution fusion | flops 810483712 | bytes 4457504 | tf_op jit(solution)/shard_map/ky,xyz->xkz/dot_general | solution.py:31
  123.8 2.7 %fusion.5 = f32[8,256,256]{2,1,0:T(8,128)S(1)} fusion(f32[8,256,256]{2,1,0:T(8,128)S(1)} %fusion.9), kind=kOutput, calls=%fused_computation.7 | convolution fusion | flops 806289408 | bytes 4194304 | tf_op jit(solution)/shard_map/kz,xyz->xyk/dot_general | solution.py:31
  126.5 2.1 %reshape.90 = f32[8,16,16,2,128]{4,3,2,1,0:T(2,128)} reshape(f32[8,256,256]{2,1,0:T(8,128)S(1)} %fusion.5) | data formatting | bytes 4194304 | tf_op jit(solution)/shard_map/reshape | solution.py:244
  128.6 3.2 %copy.25 = f32[8,16,16,2,128]{4,2,0,3,1:T(8,128)} copy(f32[8,16,16,2,128]{4,3,2,1,0:T(2,128)} %reshape.90) | data formatting | bytes 4194304 | tf_op jit(solution)/shard_map/reshape | solution.py:244
  131.8 5.3 %all-to-all-start.1 = ((f32[32,8,16,128]{3,2,1,0:T(8,128)}), f32[32,8,16,128]{3,2,1,0:T(8,128)S(1)}, u32[]{:S(2)}, u32[]{:S(2)}) async-start(f32[32,8,16,128]{3,2,1,0:T(8,128)} %bitcast.48), calls=%async_computation.1 | async-start | bytes 4194304 | tf_op jit(solution)/shard_map/all_to_all | solution.py:246
  137.1 0.0 copy-done.11
  137.1 0.2 collective-permute-start.4
  137.3 2.5 %collective-permute-start.5 = (f32[2,128,256]{2,1,0:T(8,128)S(1)}, f32[2,128,256]{2,1,0:T(8,128)S(1)}, u32[]{:S(2)}, u32[]{:S(2)}) collective-permute-start(f32[2,128,256]{2,1,0:T(8,128)S(1)} %copy-done.10), channel_id=1, source_target_pairs={{2,0},{4,2},{6,4},{8,6},{10,8},{12,10},{14,12},{16,14},{18,16},{20... | collective-permute-start | bytes 786440 | tf_op jit(solution)/shard_map/ppermute | solution.py:163
  139.8 1.5 collective-permute-start.6
  141.3 0.6 collective-permute-start.7
  141.9 11.8 %collective-permute-done.6.z_low_ref = f32[2,16,1,256]{3,2,1,0:T(1,128)S(1)} collective-permute-done((f32[2,16,1,256]{3,2,1,0:T(1,128)S(1)}, f32[2,16,1,256]{3,2,1,0:T(1,128)S(1)}, u32[]{:S(2)}, u32[]{:S(2)}) %collective-permute-start.6) | collective-permute-done | bytes 32800 | tf_op jit(solution)/shard_map/ppermute | solution.py:163
  153.7 0.7 collective-permute-done.7.z_high_ref
  154.4 33.1 %collective-permute-done.4.y_low_ref = f32[2,128,256]{2,1,0:T(8,128)S(1)} collective-permute-done((f32[2,128,256]{2,1,0:T(8,128)S(1)}, f32[2,128,256]{2,1,0:T(8,128)S(1)}, u32[]{:S(2)}, u32[]{:S(2)}) %collective-permute-start.4) | collective-permute-done | bytes 262176 | tf_op jit(solution)/shard_map/ppermute | solution.py:163
  187.4 0.0 collective-permute-done.5.y_high_ref
  187.4 0.0 copy-done.7
  187.5 0.7 copy-done.2
  188.1 0.1 copy-done.3
  188.2 6.8 %shard_map.70 = f32[2,16,128,256]{3,2,1,0:T(8,128)} custom-call(f32[2,16,128,256]{3,2,1,0:T(8,128)} %get-tuple-element.20.w_ref.w_prev.w_next, f32[2,16,128,256]{3,2,1,0:T(8,128)} %get-tuple-element.20.w_ref.w_prev.w_next, f32[2,16,128,256]{3,2,1,0:T(8,128)} %get-tuple-element.20.w_ref.w_prev.w_next, f32[2,128,256]{2,1,0:T(8,128)} %copy-done.2, ...), custom_call_target="tpu_custom_call" | custom-call | tf_op jit(solution)/shard_map/pallas_call | solution.py:206
  195.0 0.0 all-to-all-done.1
  195.0 4.3 %fusion.11 = f32[16,128,256]{2,1,0:T(8,128)} fusion(f32[256,16,128]{2,1,0:T(8,128)S(1)} %bitcast.47), kind=kOutput, calls=%fused_computation.12 | convolution fusion | flops 806813696 | bytes 4194304 | tf_op jit(solution)/shard_map/kn,nyz->yzk/dot_general | solution.py:31
  (24 shorter events, 0.1 us)
Async XLA Ops:
  14.1 4.3 %copy-start.9 = (f32[2,16,1,256]{3,2,1,0:T(1,128)S(1)}, f32[2,16,1,256]{3,2,1,0:T(1,128)}, u32[]{:S(2)}) copy-start(f32[2,16,1,256]{3,2,1,0:T(1,128)} %get-tuple-element.18) | copy-start | bytes 98308
  14.1 6.0 %copy-start.8 = (f32[2,16,1,256]{3,2,1,0:T(1,128)S(1)}, f32[2,16,1,256]{3,2,1,0:T(1,128)}, u32[]{:S(2)}) copy-start(f32[2,16,1,256]{3,2,1,0:T(1,128)} %get-tuple-element.19) | copy-start | bytes 98308
  15.1 11.0 %collective-permute-start.1 = (f32[6,128,256]{2,1,0:T(8,128)S(1)}, f32[6,128,256]{2,1,0:T(8,128)S(1)}, u32[]{:S(2)}, u32[]{:S(2)}) collective-permute-start(f32[6,128,256]{2,1,0:T(8,128)S(1)} %pad_maximum_fusion.1), channel_id=1, source_target_pairs={{2,0},{4,2},{6,4},{8,6},{10,8},{12,10},{14,12},{16,14},{18,16},{20... | collective-permute-start | bytes 2359304 | tf_op jit(solution)/shard_map/ppermute | solution.py:163
  17.0 12.5 %collective-permute-start = (f32[6,128,256]{2,1,0:T(8,128)S(1)}, f32[6,128,256]{2,1,0:T(8,128)S(1)}, u32[]{:S(2)}, u32[]{:S(2)}) collective-permute-start(f32[6,128,256]{2,1,0:T(8,128)S(1)} %pad_maximum_fusion), channel_id=1, source_target_pairs={{0,2},{2,4},{4,6},{6,8},{8,10},{10,12},{12,14},{14,16},{16,18},{18... | collective-permute-start | bytes 2359304 | tf_op jit(solution)/shard_map/ppermute | solution.py:163
  18.5 5.7 %collective-permute-start.2 = (f32[6,16,1,256]{3,2,1,0:T(1,128)S(1)}, f32[6,16,1,256]{3,2,1,0:T(1,128)S(1)}, u32[]{:S(2)}, u32[]{:S(2)}) collective-permute-start(f32[6,16,1,256]{3,2,1,0:T(1,128)S(1)} %pad_maximum_fusion.2), channel_id=1, source_target_pairs={{0,1},{1,0},{2,3},{3,2},{4,5},{5,4},{6,7},{7,6},{8,9},{9,8},{10,11... | collective-permute-start | bytes 294920 | tf_op jit(solution)/shard_map/ppermute | solution.py:163
  20.2 6.0 %collective-permute-start.3 = (f32[6,16,1,256]{3,2,1,0:T(1,128)S(1)}, f32[6,16,1,256]{3,2,1,0:T(1,128)S(1)}, u32[]{:S(2)}, u32[]{:S(2)}) collective-permute-start(f32[6,16,1,256]{3,2,1,0:T(1,128)S(1)} %pad_maximum_fusion.3), channel_id=1, source_target_pairs={{1,0},{0,1},{3,2},{2,3},{5,4},{4,5},{7,6},{6,7},{9,8},{8,9},{11,10... | collective-permute-start | bytes 294920 | tf_op jit(solution)/shard_map/ppermute | solution.py:163
  24.2 5.3 %copy-start.4 = (f32[6,16,1,256]{3,2,1,0:T(1,128)}, f32[6,16,1,256]{3,2,1,0:T(1,128)S(1)}, u32[]{:S(2)}) copy-start(f32[6,16,1,256]{3,2,1,0:T(1,128)S(1)} %collective-permute-done.2.refs_12_) | copy-start | bytes 294916
  26.2 3.3 %copy-start.5 = (f32[6,16,1,256]{3,2,1,0:T(1,128)}, f32[6,16,1,256]{3,2,1,0:T(1,128)S(1)}, u32[]{:S(2)}) copy-start(f32[6,16,1,256]{3,2,1,0:T(1,128)S(1)} %collective-permute-done.3.refs_13_) | copy-start | bytes 294916
  26.2 3.3 %copy-start = (f32[6,128,256]{2,1,0:T(8,128)}, f32[6,128,256]{2,1,0:T(8,128)S(1)}, u32[]{:S(2)}) copy-start(f32[6,128,256]{2,1,0:T(8,128)S(1)} %collective-permute-done.1.refs_11_) | copy-start | bytes 2359300
  29.5 1.0 copy-start.1
  51.5 59.6 %all-to-all-start = ((f32[32,8,16,128]{3,2,1,0:T(8,128)}), f32[32,8,16,128]{3,2,1,0:T(8,128)S(1)}, u32[]{:S(2)}, u32[]{:S(2)}) async-start(f32[32,8,16,128]{3,2,1,0:T(8,128)} %copy.21), calls=%async_computation | async-start | bytes 4194304 | tf_op jit(solution)/shard_map/all_to_all | solution.py:231
  131.8 5.3 %copy-start.11 = (f32[2,128,256]{2,1,0:T(8,128)S(1)}, f32[2,128,256]{2,1,0:T(8,128)}, u32[]{:S(2)}) copy-start(f32[2,128,256]{2,1,0:T(8,128)} %get-tuple-element.21) | copy-start | bytes 786436
  131.8 5.5 %copy-start.10 = (f32[2,128,256]{2,1,0:T(8,128)S(1)}, f32[2,128,256]{2,1,0:T(8,128)}, u32[]{:S(2)}) copy-start(f32[2,128,256]{2,1,0:T(8,128)} %get-tuple-element.22) | copy-start | bytes 786436
  131.8 8.0 %copy-start.13 = (f32[2,16,1,256]{3,2,1,0:T(1,128)S(1)}, f32[2,16,1,256]{3,2,1,0:T(1,128)}, u32[]{:S(2)}) copy-start(f32[2,16,1,256]{3,2,1,0:T(1,128)} %get-tuple-element.23) | copy-start | bytes 98308
  131.8 9.5 %copy-start.12 = (f32[2,16,1,256]{3,2,1,0:T(1,128)S(1)}, f32[2,16,1,256]{3,2,1,0:T(1,128)}, u32[]{:S(2)}) copy-start(f32[2,16,1,256]{3,2,1,0:T(1,128)} %get-tuple-element.24) | copy-start | bytes 98308
  131.8 63.2 %all-to-all-start.1 = ((f32[32,8,16,128]{3,2,1,0:T(8,128)}), f32[32,8,16,128]{3,2,1,0:T(8,128)S(1)}, u32[]{:S(2)}, u32[]{:S(2)}) async-start(f32[32,8,16,128]{3,2,1,0:T(8,128)} %bitcast.48), calls=%async_computation.1 | async-start | bytes 4194304 | tf_op jit(solution)/shard_map/all_to_all | solution.py:246
  137.1 50.3 %collective-permute-start.4 = (f32[2,128,256]{2,1,0:T(8,128)S(1)}, f32[2,128,256]{2,1,0:T(8,128)S(1)}, u32[]{:S(2)}, u32[]{:S(2)}) collective-permute-start(f32[2,128,256]{2,1,0:T(8,128)S(1)} %copy-done.11), channel_id=1, source_target_pairs={{0,2},{2,4},{4,6},{6,8},{8,10},{10,12},{12,14},{14,16},{16,18},{18... | collective-permute-start | bytes 786440 | tf_op jit(solution)/shard_map/ppermute | solution.py:163
  137.3 50.1 %collective-permute-start.5 = (f32[2,128,256]{2,1,0:T(8,128)S(1)}, f32[2,128,256]{2,1,0:T(8,128)S(1)}, u32[]{:S(2)}, u32[]{:S(2)}) collective-permute-start(f32[2,128,256]{2,1,0:T(8,128)S(1)} %copy-done.10), channel_id=1, source_target_pairs={{2,0},{4,2},{6,4},{8,6},{10,8},{12,10},{14,12},{16,14},{18,16},{20... | collective-permute-start | bytes 786440 | tf_op jit(solution)/shard_map/ppermute | solution.py:163
  139.8 13.8 %collective-permute-start.6 = (f32[2,16,1,256]{3,2,1,0:T(1,128)S(1)}, f32[2,16,1,256]{3,2,1,0:T(1,128)S(1)}, u32[]{:S(2)}, u32[]{:S(2)}) collective-permute-start(f32[2,16,1,256]{3,2,1,0:T(1,128)S(1)} %copy-done.13), channel_id=1, source_target_pairs={{0,1},{1,0},{2,3},{3,2},{4,5},{5,4},{6,7},{7,6},{8,9},{9,8},{10,11... | collective-permute-start | bytes 98312 | tf_op jit(solution)/shard_map/ppermute | solution.py:163
  141.3 13.1 %collective-permute-start.7 = (f32[2,16,1,256]{3,2,1,0:T(1,128)S(1)}, f32[2,16,1,256]{3,2,1,0:T(1,128)S(1)}, u32[]{:S(2)}, u32[]{:S(2)}) collective-permute-start(f32[2,16,1,256]{3,2,1,0:T(1,128)S(1)} %copy-done.12), channel_id=1, source_target_pairs={{1,0},{0,1},{3,2},{2,3},{5,4},{4,5},{7,6},{6,7},{9,8},{8,9},{11,10... | collective-permute-start | bytes 98312 | tf_op jit(solution)/shard_map/ppermute | solution.py:163
  153.7 33.8 %copy-start.6 = (f32[2,16,1,256]{3,2,1,0:T(1,128)}, f32[2,16,1,256]{3,2,1,0:T(1,128)S(1)}, u32[]{:S(2)}) copy-start(f32[2,16,1,256]{3,2,1,0:T(1,128)S(1)} %collective-permute-done.6.z_low_ref) | copy-start | bytes 98308
  154.4 33.1 %copy-start.7 = (f32[2,16,1,256]{3,2,1,0:T(1,128)}, f32[2,16,1,256]{3,2,1,0:T(1,128)S(1)}, u32[]{:S(2)}) copy-start(f32[2,16,1,256]{3,2,1,0:T(1,128)S(1)} %collective-permute-done.7.z_high_ref) | copy-start | bytes 98308
  187.4 0.7 copy-start.2
  187.4 0.8 copy-start.3
where the time goes:
time: 200 us; the launch traced here: 199 us
  waiting for transfers between devices  101 us (50%)
  Pallas kernels  33.7 us (17%)
  starting transfers between devices  25.7 us (13%)
  local copies, waits for them, and re-layouts  18.1 us (9%)
  matrix products  17.4 us (9%)
  other arithmetic  2.32 us (1%)
    ppermute x4, waiting for transfers between devices, send_edges(): lax.ppermute(last, axis, up)  51.7 us
    all_to_all x2, waiting for transfers between devices, dipole_adjoint(): spec = lax.all_to_all(spec, ('gy', 'gz'), 0, 0, tiled=True)  47 us
    all_to_all x2, starting transfers between devices, dipole_adjoint(): spec = lax.all_to_all(spec, ('gy', 'gz'), 0, 0, tiled=True)  17.8 us
    dot_general x6, matrix products, along(): return jnp.einsum(spec, table, values, precision=lax.Precision.HIGH)  17.4 us
    pallas_call x1, Pallas kernels, backward_sections(): pl.pallas_call(functools.partial(first_kernel, rows=rows), grid=grid, in_...  14.8 us
    pallas_call x1, Pallas kernels, backward_sections(): pl.pallas_call(functools.partial(factor_kernel, rows=rows), grid=grid, in...  12.2 us
    pallas_call x1, Pallas kernels, backward_sections(): pl.pallas_call(functools.partial(second_kernel, rows=rows), grid=grid, in...  6.77 us
    reshape x2, local copies, waits for them, and re-layouts, dipole_adjoint(): spec = spec.reshape(block_x, count_y, block_y, count_z, block_z)  5.3 us
  transfers between devices with their start and end apart: 10, of which 7 were waited for; matrix products, arithmetic and copies ran while one was open for 1% of the time, Pallas kernels for 3%

commit v1 on v0

--- a/solution.py
+++ b/solution.py
@@ -103,17 +103,20 @@
 
 def first_kernel(*refs, rows):
     (mm_ref, mm_prev, mm_next, ms_ref, ms_prev, ms_next, w_ref, w_prev, w_next,
-     factor_ref, y_low_ref, y_high_ref, z_low_ref, z_high_ref, pg_ref, w2_ref) = refs[:16]
+     factor_ref, *halo_refs) = refs[:18]
+    pg_ref, w2_ref = refs[18:20]
     step = pl.program_id(0)
     fields = ((mm_ref, mm_prev, mm_next), (ms_ref, ms_prev, ms_next), (w_ref, w_prev, w_next))
     for r in range(rows):
         new = []
         for f, (cur, prev, nxt) in enumerate(fields):
+            y_low_ref, y_high_ref, z_low_ref, z_high_ref = halo_refs[4 * (f // 2):4 * (f // 2) + 4]
             pair = []
             for comp in range(2):
-                below, above = neighbour_planes(cur, prev, nxt, y_low_ref, y_high_ref, rows, 2 * f + comp, comp, r)
+                index = 2 * f + comp if f < 2 else comp
+                below, above = neighbour_planes(cur, prev, nxt, y_low_ref, y_high_ref, rows, index, comp, r)
                 pair.append(plane_update(cur[comp, r], below, above,
-                                         z_low_ref[2 * f + comp, r], z_high_ref[2 * f + comp, r]))
+                                         z_low_ref[index, r], z_high_ref[index, r]))
             new.append(pair)
         (u1_real, u1_imag), (u2_real, u2_imag), (lam_real, lam_imag) = new
         w_real = w_ref[0, r]
@@ -126,7 +129,7 @@
         pg_ref[r] = grad + (w2_real * u2_imag - w2_imag * u2_real)
         w2_ref[0, r] = w2_real
         w2_ref[1, r] = w2_imag
-        write_edges(step, rows, r, [w2_real, w2_imag], *refs[16:])
+        write_edges(step, rows, r, [w2_real, w2_imag], *refs[20:])
 
 
 def second_kernel(w_ref, w_prev, w_next, y_low_ref, y_high_ref, z_low_ref, z_high_ref, out_ref, *, rows):
@@ -190,18 +193,19 @@
         out_specs=[cur, cur] + edge_specs,
         out_shape=[pair, pair] + edge_shapes,
     )(adjoint_end, phase, labels)
-    mag_edges = input_edges([mag_middle, mag_start])
-    halos = send_edges(*[jnp.concatenate([a, b]) for a, b in zip(mag_edges, w_edges)])
+    mag_halos = send_edges(*input_edges([mag_middle, mag_start]))
+    w_halos = send_edges(*w_edges)
     phase_grad, w_second, *w2_edges = pl.pallas_call(
         functools.partial(first_kernel, rows=rows),
         grid=grid,
         in_specs=field_specs(mag_middle.shape, rows) + field_specs(mag_start.shape, rows)
         + field_specs(w_first.shape, rows)
-        + [cur, whole((6, length_z, length_x)), whole((6, length_z, length_x)), zspec(6), zspec(6)],
+        + [cur, whole((4, length_z, length_x)), whole((4, length_z, length_x)), zspec(4), zspec(4),
+           whole((2, length_z, length_x)), whole((2, length_z, length_x)), zspec(2), zspec(2)],
         out_specs=[cur_plane, cur] + edge_specs,
         out_shape=[plane, pair] + edge_shapes,
     )(mag_middle, mag_middle, mag_middle, mag_start, mag_start, mag_start,
-      w_first, w_first, w_first, factor, *halos)
+      w_first, w_first, w_first, factor, *mag_halos, *w_halos)
     halos = send_edges(*w2_edges)
     lam = pl.pallas_call(
         functools.partial(second_kernel, rows=rows),

time: 200 us -> 200 us (level)
  other arithmetic: 2.32 us -> 0.31 us
    ppermute x4 -> x6, starting transfers between devices: 4.55 us -> 11.3 us  [send_edges(): lax.ppermute(first, axis, down)]
    all_to_all x2, starting transfers between devices: 17.8 us -> 11.1 us  [dipole_adjoint(): spec = lax.all_to_all(spec, ('gy', 'gz'), 0, 0, tiled=True)]
    ppermute x4 -> x6, waiting for transfers between devices: 2.62 us -> 6.05 us  [send_edges(): lax.ppermute(first, axis, down)]
    ppermute x4 -> x6, waiting for transfers between devices: 51.7 us -> 49.2 us  [send_edges(): lax.ppermute(last, axis, up)]
    concatenate x4, other arithmetic: 2.2 us -> 0.19 us  [the longest x1 0.06 us: input_edges(): z_last = jnp.concatenate([f[:, :, -1:] for f in fields])]
    ppermute x4 -> x6, starting transfers between devices: 3.28 us -> 4.76 us  [send_edges(): lax.ppermute(last, axis, up)]
  transfers between devices with their start and end apart: 10 -> 14, of which waited for: 7 -> 8; matrix products, arithmetic and copies ran while one was open for 1% -> 1% of each run, Pallas kernels for 3% -> 9%
where the time goes in v1:
time: 200 us
  waiting for transfers between devices  102 us (51%)
  Pallas kernels  33.7 us (17%)
  starting transfers between devices  27.2 us (14%)
  local copies, waits for them, and re-layouts  18.2 us (9%)
  matrix products  17.4 us (9%)
    ppermute x6, waiting for transfers between devices, send_edges(): lax.ppermute(last, axis, up)  49.2 us
    all_to_all x2, waiting for transfers between devices, dipole_adjoint(): spec = lax.all_to_all(spec, ('gy', 'gz'), 0, 0, tiled=True)  46.9 us
    dot_general x6, matrix products, along(): return jnp.einsum(spec, table, values, precision=lax.Precision.HIGH)  17.4 us
    pallas_call x1, Pallas kernels, backward_sections(): pl.pallas_call(functools.partial(first_kernel, rows=rows), grid=grid, in_...  14.8 us
    pallas_call x1, Pallas kernels, backward_sections(): pl.pallas_call(functools.partial(factor_kernel, rows=rows), grid=grid, in...  12.1 us
    ppermute x6, starting transfers between devices, send_edges(): lax.ppermute(first, axis, down)  11.3 us
    all_to_all x2, starting transfers between devices, dipole_adjoint(): spec = lax.all_to_all(spec, ('gy', 'gz'), 0, 0, tiled=True)  11.1 us
    pallas_call x1, Pallas kernels, backward_sections(): pl.pallas_call(functools.partial(second_kernel, rows=rows), grid=grid, in...  6.76 us
  transfers between devices with their start and end apart: 14, of which 8 were waited for; matrix products, arithmetic and copies ran while one was open for 1% of the time, Pallas kernels for 9%

profile of v1, /device:TPU:16, one launch (start us, length us, event | category | flops | bytes accessed | tf_op | source)
XLA Modules:
  0.0 199.8 jit_solution(11828014447767264017)
XLA Ops:
  0.6 1.3 slice_bitcast_fusion
  1.9 0.1 collective-permute-start
  2.1 2.7 %collective-permute-start.1 = (f32[4,128,256]{2,1,0:T(8,128)S(1)}, f32[4,128,256]{2,1,0:T(8,128)S(1)}, u32[]{:S(2)}, u32[]{:S(2)}) collective-permute-start(f32[4,128,256]{2,1,0:T(8,128)S(1)} %pad_maximum_fusion.1), channel_id=1, source_target_pairs={{2,0},{4,2},{6,4},{8,6},{10,8},{12,10},{14,12},{16,14},{18,16},{20... | collective-permute-start | bytes 1572872 | tf_op jit(solution)/shard_map/ppermute | solution.py:166
  4.7 12.1 %shard_map.68 = (f32[2,16,128,256]{3,2,1,0:T(8,128)}, f32[2,16,128,256]{3,2,1,0:T(8,128)}, f32[2,128,256]{2,1,0:T(8,128)}, f32[2,128,256]{2,1,0:T(8,128)}, f32[2...) custom-call(f32[2,16,128,256]{3,2,1,0:T(8,128)} %lam_ref.1, f32[16,128,256]{2,1,0:T(8,128)} %phase_ref.1, ...), custom_call_target="tpu_custom_call" | custom-call | tf_op jit(solution)/shard_map/pallas_call | solution.py:189
  16.9 0.1 collective-permute-start.4
  16.9 2.6 %collective-permute-start.5 = (f32[2,128,256]{2,1,0:T(8,128)}, f32[2,128,256]{2,1,0:T(8,128)S(1)}, u32[]{:S(2)}, u32[]{:S(2)}) collective-permute-start(f32[2,128,256]{2,1,0:T(8,128)} %get-tuple-element.17), channel_id=1, source_target_pairs={{2,0},{4,2},{6,4},{8,6},{10,8},{12,10},{14,12},{16,14},{18,16},{20... | collective-permute-start | bytes 786440 | tf_op jit(solution)/shard_map/ppermute | solution.py:166
  19.6 1.5 collective-permute-start.6
  21.1 1.3 fusion.65
  22.4 1.6 collective-permute-done.6.refs_16_
  23.9 1.5 collective-permute-start.7
  25.4 0.1 pad_maximum_fusion.2
  25.5 2.6 %collective-permute-done.7.refs_17_ = f32[2,16,1,256]{3,2,1,0:T(1,128)S(1)} collective-permute-done((f32[2,16,1,256]{3,2,1,0:T(1,128)}, f32[2,16,1,256]{3,2,1,0:T(1,128)S(1)}, u32[]{:S(2)}, u32[]{:S(2)}) %collective-permute-start.7) | collective-permute-done | bytes 32800 | tf_op jit(solution)/shard_map/ppermute | solution.py:166
  28.1 1.5 collective-permute-start.2
  29.6 0.1 pad_maximum_fusion.3
  29.6 2.7 %collective-permute-done.2.refs_12_ = f32[4,16,1,256]{3,2,1,0:T(1,128)S(1)} collective-permute-done((f32[4,16,1,256]{3,2,1,0:T(1,128)S(1)}, f32[4,16,1,256]{3,2,1,0:T(1,128)S(1)}, u32[]{:S(2)}, u32[]{:S(2)}) %collective-permute-start.2) | collective-permute-done | bytes 65568 | tf_op jit(solution)/shard_map/ppermute | solution.py:166
  32.3 1.5 collective-permute-start.3
  33.8 2.8 %collective-permute-done.3.refs_13_ = f32[4,16,1,256]{3,2,1,0:T(1,128)S(1)} collective-permute-done((f32[4,16,1,256]{3,2,1,0:T(1,128)S(1)}, f32[4,16,1,256]{3,2,1,0:T(1,128)S(1)}, u32[]{:S(2)}, u32[]{:S(2)}) %collective-permute-start.3) | collective-permute-done | bytes 65568 | tf_op jit(solution)/shard_map/ppermute | solution.py:166
  36.7 0.5 copy-done.7
  37.2 0.1 copy-done.2
  37.3 0.1 copy-done.3
  37.4 0.2 copy-done
  37.6 0.2 copy-done.1
  37.8 14.8 %shard_map.69 = (f32[16,128,256]{2,1,0:T(8,128)}, f32[2,16,128,256]{3,2,1,0:T(8,128)}, f32[2,128,256]{2,1,0:T(8,128)}, f32[2,128,256]{2,1,0:T(8,128)}, f32[2,16,...) custom-call(f32[2,16,128,256]{3,2,1,0:T(8,128)} %refs_2_.1, f32[2,16,128,256]{3,2,1,0:T(8,128)} %refs_2_.1, ...), custom_call_target="tpu_custom_call" | custom-call | tf_op jit(solution)/shard_map/pallas_call | solution.py:198
  52.6 3.7 %convolution_bitcast_fusion = f32[32,8,16,128]{3,1,0,2:T(8,128)S(1)} fusion(f32[16,128,256]{2,1,0:T(8,128)} %get-tuple-element.25), kind=kOutput, calls=%fused_computation.13 | convolution fusion | flops 806289408 | bytes 4194304 | tf_op jit(solution)/shard_map/kn,yzn->kyz/dot_general | solution.py:31
  56.3 2.5 %copy.21 = f32[32,8,16,128]{3,2,1,0:T(8,128)} copy(f32[32,8,16,128]{3,1,0,2:T(8,128)S(1)} %convolution_bitcast_fusion) | data formatting | bytes 4194304 | tf_op jit(solution)/shard_map/reshape | solution.py:234
  58.8 5.8 %all-to-all-start = ((f32[32,8,16,128]{3,2,1,0:T(8,128)}), f32[32,8,16,128]{3,2,1,0:T(8,128)S(1)}, u32[]{:S(2)}, u32[]{:S(2)}) async-start(f32[32,8,16,128]{3,2,1,0:T(8,128)} %copy.21), calls=%async_computation | async-start | bytes 4194304 | tf_op jit(solution)/shard_map/all_to_all | solution.py:235
  64.6 0.1 broadcast_add_fusion
  64.7 46.9 %all-to-all-done = f32[32,8,16,128]{3,2,1,0:T(8,128)S(1)} async-done(((f32[32,8,16,128]{3,2,1,0:T(8,128)}), f32[32,8,16,128]{3,2,1,0:T(8,128)S(1)}, u32[]{:S(2)}, u32[]{:S(2)}) %all-to-all-start) | async-done | bytes 2097184 | tf_op jit(solution)/shard_map/all_to_all | solution.py:235
  111.6 2.9 %copy.22 = f32[8,16,16,2,128]{4,3,2,1,0:T(2,128)} copy(f32[8,16,16,2,128]{4,2,0,3,1:T(8,128)S(1)} %bitcast.49) | data formatting | bytes 4194304 | tf_op jit(solution)/shard_map/transpose | solution.py:237
  114.5 2.9 %reshape.89 = f32[8,256,256]{2,1,0:T(8,128)S(1)} reshape(f32[8,16,16,2,128]{4,3,2,1,0:T(2,128)} %copy.22) | data formatting | bytes 4194304 | tf_op jit(solution)/shard_map/reshape | solution.py:237
  117.5 2.1 %fusion.29 = f32[8,256,256]{1,2,0:T(8,128)S(1)} fusion(f32[8,256,256]{2,1,0:T(8,128)S(1)} %reshape.89), kind=kOutput, calls=%fused_computation.34 | convolution fusion | flops 806289408 | bytes 4194304 | tf_op jit(solution)/shard_map/kz,xyz->xyk/dot_general | solution.py:31
  119.5 2.1 %fusion.27 = f32[8,256,256]{2,1,0:T(8,128)S(1)} fusion(f32[8,256,256]{1,2,0:T(8,128)S(1)} %fusion.29), kind=kOutput, calls=%fused_computation.32 | convolution fusion | flops 806289408 | bytes 4194304 | tf_op jit(solution)/shard_map/ky,xyz->xkz/dot_general | solution.py:31
  121.6 2.6 %fusion.9 = f32[8,256,256]{2,1,0:T(8,128)S(1)} fusion(f32[8,256,256]{2,1,0:T(8,128)S(1)} %fusion.27, f32[256]{0:T(256)S(1)} %fusion.37, s32[8]{0:T(128)S(1)} %fusion.36, s32[256,256]{0,1:T(8,128)S(1)} %broadcast_add_fusion), kind=kOutput, calls=%fused_computation.11 | convolution fusion | flops 810483712 | bytes 4457504 | tf_op jit(solution)/shard_map/ky,xyz->xkz/dot_general | solution.py:31
  124.2 2.7 %fusion.5 = f32[8,256,256]{2,1,0:T(8,128)S(1)} fusion(f32[8,256,256]{2,1,0:T(8,128)S(1)} %fusion.9), kind=kOutput, calls=%fused_computation.7 | convolution fusion | flops 806289408 | bytes 4194304 | tf_op jit(solution)/shard_map/kz,xyz->xyk/dot_general | solution.py:31
  126.9 2.1 %reshape.90 = f32[8,16,16,2,128]{4,3,2,1,0:T(2,128)} reshape(f32[8,256,256]{2,1,0:T(8,128)S(1)} %fusion.5) | data formatting | bytes 4194304 | tf_op jit(solution)/shard_map/reshape | solution.py:248
  129.0 3.2 %copy.25 = f32[8,16,16,2,128]{4,2,0,3,1:T(8,128)} copy(f32[8,16,16,2,128]{4,3,2,1,0:T(2,128)} %reshape.90) | data formatting | bytes 4194304 | tf_op jit(solution)/shard_map/reshape | solution.py:248
  132.3 5.3 %all-to-all-start.1 = ((f32[32,8,16,128]{3,2,1,0:T(8,128)}), f32[32,8,16,128]{3,2,1,0:T(8,128)S(1)}, u32[]{:S(2)}, u32[]{:S(2)}) async-start(f32[32,8,16,128]{3,2,1,0:T(8,128)} %bitcast.48), calls=%async_computation.1 | async-start | bytes 4194304 | tf_op jit(solution)/shard_map/all_to_all | solution.py:250
  137.6 0.2 collective-permute-start.8
  137.8 2.5 %collective-permute-start.9 = (f32[2,128,256]{2,1,0:T(8,128)S(1)}, f32[2,128,256]{2,1,0:T(8,128)S(1)}, u32[]{:S(2)}, u32[]{:S(2)}) collective-permute-start(f32[2,128,256]{2,1,0:T(8,128)S(1)} %copy-done.12), channel_id=1, source_target_pairs={{2,0},{4,2},{6,4},{8,6},{10,8},{12,10},{14,12},{16,14},{18,16},{20... | collective-permute-start | bytes 786440 | tf_op jit(solution)/shard_map/ppermute | solution.py:166
  140.3 1.5 collective-permute-start.10
  141.7 0.6 collective-permute-start.11
  142.3 11.8 %collective-permute-done.10.z_low_ref = f32[2,16,1,256]{3,2,1,0:T(1,128)S(1)} collective-permute-done((f32[2,16,1,256]{3,2,1,0:T(1,128)S(1)}, f32[2,16,1,256]{3,2,1,0:T(1,128)S(1)}, u32[]{:S(2)}, u32[]{:S(2)}) %collective-permute-start.10) | collective-permute-done | bytes 32800 | tf_op jit(solution)/shard_map/ppermute | solution.py:166
  154.1 0.7 collective-permute-done.11.z_high_ref
  154.8 33.1 %collective-permute-done.8.y_low_ref = f32[2,128,256]{2,1,0:T(8,128)S(1)} collective-permute-done((f32[2,128,256]{2,1,0:T(8,128)S(1)}, f32[2,128,256]{2,1,0:T(8,128)S(1)}, u32[]{:S(2)}, u32[]{:S(2)}) %collective-permute-start.8) | collective-permute-done | bytes 262176 | tf_op jit(solution)/shard_map/ppermute | solution.py:166
  187.9 0.7 copy-done.4
  188.6 0.1 copy-done.5
  188.7 6.8 %shard_map.70 = f32[2,16,128,256]{3,2,1,0:T(8,128)} custom-call(f32[2,16,128,256]{3,2,1,0:T(8,128)} %get-tuple-element.20.w_ref.w_prev.w_next, f32[2,16,128,256]{3,2,1,0:T(8,128)} %get-tuple-element.20.w_ref.w_prev.w_next, f32[2,16,128,256]{3,2,1,0:T(8,128)} %get-tuple-element.20.w_ref.w_prev.w_next, f32[2,128,256]{2,1,0:T(8,128)} %copy-done.4, ...), custom_call_target="tpu_custom_call" | custom-call | tf_op jit(solution)/shard_map/pallas_call | solution.py:210
  195.4 4.3 %fusion.11 = f32[16,128,256]{2,1,0:T(8,128)} fusion(f32[256,16,128]{2,1,0:T(8,128)S(1)} %bitcast.47), kind=kOutput, calls=%fused_computation.12 | convolution fusion | flops 806813696 | bytes 4194304 | tf_op jit(solution)/shard_map/kn,nyz->yzk/dot_general | solution.py:31
  (36 shorter events, 0.2 us)
Async XLA Ops:
  1.9 34.7 %collective-permute-start = (f32[4,128,256]{2,1,0:T(8,128)S(1)}, f32[4,128,256]{2,1,0:T(8,128)S(1)}, u32[]{:S(2)}, u32[]{:S(2)}) collective-permute-start(f32[4,128,256]{2,1,0:T(8,128)S(1)} %pad_maximum_fusion), channel_id=1, source_target_pairs={{0,2},{2,4},{4,6},{6,8},{8,10},{10,12},{12,14},{14,16},{16,18},{18... | collective-permute-start | bytes 1572872 | tf_op jit(solution)/shard_map/ppermute | solution.py:166
  2.1 34.6 %collective-permute-start.1 = (f32[4,128,256]{2,1,0:T(8,128)S(1)}, f32[4,128,256]{2,1,0:T(8,128)S(1)}, u32[]{:S(2)}, u32[]{:S(2)}) collective-permute-start(f32[4,128,256]{2,1,0:T(8,128)S(1)} %pad_maximum_fusion.1), channel_id=1, source_target_pairs={{2,0},{4,2},{6,4},{8,6},{10,8},{12,10},{14,12},{16,14},{18,16},{20... | collective-permute-start | bytes 1572872 | tf_op jit(solution)/shard_map/ppermute | solution.py:166
  16.9 19.7 %collective-permute-start.4 = (f32[2,128,256]{2,1,0:T(8,128)}, f32[2,128,256]{2,1,0:T(8,128)S(1)}, u32[]{:S(2)}, u32[]{:S(2)}) collective-permute-start(f32[2,128,256]{2,1,0:T(8,128)} %get-tuple-element.16), channel_id=1, source_target_pairs={{0,2},{2,4},{4,6},{6,8},{8,10},{10,12},{12,14},{14,16},{16,18},{18... | collective-permute-start | bytes 786440 | tf_op jit(solution)/shard_map/ppermute | solution.py:166
  16.9 19.7 %collective-permute-start.5 = (f32[2,128,256]{2,1,0:T(8,128)}, f32[2,128,256]{2,1,0:T(8,128)S(1)}, u32[]{:S(2)}, u32[]{:S(2)}) collective-permute-start(f32[2,128,256]{2,1,0:T(8,128)} %get-tuple-element.17), channel_id=1, source_target_pairs={{2,0},{4,2},{6,4},{8,6},{10,8},{12,10},{14,12},{16,14},{18,16},{20... | collective-permute-start | bytes 786440 | tf_op jit(solution)/shard_map/ppermute | solution.py:166
  19.6 4.4 %collective-permute-start.6 = (f32[2,16,1,256]{3,2,1,0:T(1,128)}, f32[2,16,1,256]{3,2,1,0:T(1,128)S(1)}, u32[]{:S(2)}, u32[]{:S(2)}) collective-permute-start(f32[2,16,1,256]{3,2,1,0:T(1,128)} %get-tuple-element.18), channel_id=1, source_target_pairs={{0,1},{1,0},{2,3},{3,2},{4,5},{5,4},{6,7},{7,6},{8,9},{9,8},{10,11... | collective-permute-start | bytes 98312 | tf_op jit(solution)/shard_map/ppermute | solution.py:166
  23.9 12.7 %copy-start.10 = (f32[2,16,1,256]{3,2,1,0:T(1,128)}, f32[2,16,1,256]{3,2,1,0:T(1,128)S(1)}, u32[]{:S(2)}) copy-start(f32[2,16,1,256]{3,2,1,0:T(1,128)S(1)} %collective-permute-done.6.refs_16_) | copy-start | bytes 98308
  23.9 4.1 %collective-permute-start.7 = (f32[2,16,1,256]{3,2,1,0:T(1,128)}, f32[2,16,1,256]{3,2,1,0:T(1,128)S(1)}, u32[]{:S(2)}, u32[]{:S(2)}) collective-permute-start(f32[2,16,1,256]{3,2,1,0:T(1,128)} %get-tuple-element.19), channel_id=1, source_target_pairs={{1,0},{0,1},{3,2},{2,3},{5,4},{4,5},{7,6},{6,7},{9,8},{8,9},{11,10... | collective-permute-start | bytes 98312 | tf_op jit(solution)/shard_map/ppermute | solution.py:166
  28.1 8.6 %copy-start.11 = (f32[2,16,1,256]{3,2,1,0:T(1,128)}, f32[2,16,1,256]{3,2,1,0:T(1,128)S(1)}, u32[]{:S(2)}) copy-start(f32[2,16,1,256]{3,2,1,0:T(1,128)S(1)} %collective-permute-done.7.refs_17_) | copy-start | bytes 98308
  28.1 4.3 %collective-permute-start.2 = (f32[4,16,1,256]{3,2,1,0:T(1,128)S(1)}, f32[4,16,1,256]{3,2,1,0:T(1,128)S(1)}, u32[]{:S(2)}, u32[]{:S(2)}) collective-permute-start(f32[4,16,1,256]{3,2,1,0:T(1,128)S(1)} %pad_maximum_fusion.2), channel_id=1, source_target_pairs={{0,1},{1,0},{2,3},{3,2},{4,5},{5,4},{6,7},{7,6},{8,9},{9,8},{10,11... | collective-permute-start | bytes 196616 | tf_op jit(solution)/shard_map/ppermute | solution.py:166
  32.3 4.4 %copy-start.6 = (f32[4,16,1,256]{3,2,1,0:T(1,128)}, f32[4,16,1,256]{3,2,1,0:T(1,128)S(1)}, u32[]{:S(2)}) copy-start(f32[4,16,1,256]{3,2,1,0:T(1,128)S(1)} %collective-permute-done.2.refs_12_) | copy-start | bytes 196612
  32.3 4.3 %collective-permute-start.3 = (f32[4,16,1,256]{3,2,1,0:T(1,128)S(1)}, f32[4,16,1,256]{3,2,1,0:T(1,128)S(1)}, u32[]{:S(2)}, u32[]{:S(2)}) collective-permute-start(f32[4,16,1,256]{3,2,1,0:T(1,128)S(1)} %pad_maximum_fusion.3), channel_id=1, source_target_pairs={{1,0},{0,1},{3,2},{2,3},{5,4},{4,5},{7,6},{6,7},{9,8},{8,9},{11,10... | collective-permute-start | bytes 196616 | tf_op jit(solution)/shard_map/ppermute | solution.py:166
  36.6 0.6 copy-start.7
  36.6 0.7 copy-start.2
  36.6 0.8 copy-start.3
  36.6 1.0 copy-start
  36.7 1.2 copy-start.1
  58.8 52.8 %all-to-all-start = ((f32[32,8,16,128]{3,2,1,0:T(8,128)}), f32[32,8,16,128]{3,2,1,0:T(8,128)S(1)}, u32[]{:S(2)}, u32[]{:S(2)}) async-start(f32[32,8,16,128]{3,2,1,0:T(8,128)} %copy.21), calls=%async_computation | async-start | bytes 4194304 | tf_op jit(solution)/shard_map/all_to_all | solution.py:235
  132.2 5.3 %copy-start.13 = (f32[2,128,256]{2,1,0:T(8,128)S(1)}, f32[2,128,256]{2,1,0:T(8,128)}, u32[]{:S(2)}) copy-start(f32[2,128,256]{2,1,0:T(8,128)} %get-tuple-element.21) | copy-start | bytes 786436
  132.2 5.5 %copy-start.12 = (f32[2,128,256]{2,1,0:T(8,128)S(1)}, f32[2,128,256]{2,1,0:T(8,128)}, u32[]{:S(2)}) copy-start(f32[2,128,256]{2,1,0:T(8,128)} %get-tuple-element.22) | copy-start | bytes 786436
  132.2 8.0 %copy-start.15 = (f32[2,16,1,256]{3,2,1,0:T(1,128)S(1)}, f32[2,16,1,256]{3,2,1,0:T(1,128)}, u32[]{:S(2)}) copy-start(f32[2,16,1,256]{3,2,1,0:T(1,128)} %get-tuple-element.23) | copy-start | bytes 98308
  132.2 9.5 %copy-start.14 = (f32[2,16,1,256]{3,2,1,0:T(1,128)S(1)}, f32[2,16,1,256]{3,2,1,0:T(1,128)}, u32[]{:S(2)}) copy-start(f32[2,16,1,256]{3,2,1,0:T(1,128)} %get-tuple-element.24) | copy-start | bytes 98308
  132.3 63.2 %all-to-all-start.1 = ((f32[32,8,16,128]{3,2,1,0:T(8,128)}), f32[32,8,16,128]{3,2,1,0:T(8,128)S(1)}, u32[]{:S(2)}, u32[]{:S(2)}) async-start(f32[32,8,16,128]{3,2,1,0:T(8,128)} %bitcast.48), calls=%async_computation.1 | async-start | bytes 4194304 | tf_op jit(solution)/shard_map/all_to_all | solution.py:250
  137.6 50.3 %collective-permute-start.8 = (f32[2,128,256]{2,1,0:T(8,128)S(1)}, f32[2,128,256]{2,1,0:T(8,128)S(1)}, u32[]{:S(2)}, u32[]{:S(2)}) collective-permute-start(f32[2,128,256]{2,1,0:T(8,128)S(1)} %copy-done.13), channel_id=1, source_target_pairs={{0,2},{2,4},{4,6},{6,8},{8,10},{10,12},{12,14},{14,16},{16,18},{18... | collective-permute-start | bytes 786440 | tf_op jit(solution)/shard_map/ppermute | solution.py:166
  137.8 50.1 %collective-permute-start.9 = (f32[2,128,256]{2,1,0:T(8,128)S(1)}, f32[2,128,256]{2,1,0:T(8,128)S(1)}, u32[]{:S(2)}, u32[]{:S(2)}) collective-permute-start(f32[2,128,256]{2,1,0:T(8,128)S(1)} %copy-done.12), channel_id=1, source_target_pairs={{2,0},{4,2},{6,4},{8,6},{10,8},{12,10},{14,12},{16,14},{18,16},{20... | collective-permute-start | bytes 786440 | tf_op jit(solution)/shard_map/ppermute | solution.py:166
  140.3 13.8 %collective-permute-start.10 = (f32[2,16,1,256]{3,2,1,0:T(1,128)S(1)}, f32[2,16,1,256]{3,2,1,0:T(1,128)S(1)}, u32[]{:S(2)}, u32[]{:S(2)}) collective-permute-start(f32[2,16,1,256]{3,2,1,0:T(1,128)S(1)} %copy-done.15), channel_id=1, source_target_pairs={{0,1},{1,0},{2,3},{3,2},{4,5},{5,4},{6,7},{7,6},{8,9},{9,8},{10,11... | collective-permute-start | bytes 98312 | tf_op jit(solution)/shard_map/ppermute | solution.py:166
  141.7 13.1 %collective-permute-start.11 = (f32[2,16,1,256]{3,2,1,0:T(1,128)S(1)}, f32[2,16,1,256]{3,2,1,0:T(1,128)S(1)}, u32[]{:S(2)}, u32[]{:S(2)}) collective-permute-start(f32[2,16,1,256]{3,2,1,0:T(1,128)S(1)} %copy-done.14), channel_id=1, source_target_pairs={{1,0},{0,1},{3,2},{2,3},{5,4},{4,5},{7,6},{6,7},{9,8},{8,9},{11,10... | collective-permute-start | bytes 98312 | tf_op jit(solution)/shard_map/ppermute | solution.py:166
  154.1 33.8 %copy-start.8 = (f32[2,16,1,256]{3,2,1,0:T(1,128)}, f32[2,16,1,256]{3,2,1,0:T(1,128)S(1)}, u32[]{:S(2)}) copy-start(f32[2,16,1,256]{3,2,1,0:T(1,128)S(1)} %collective-permute-done.10.z_low_ref) | copy-start | bytes 98308
  154.8 33.1 %copy-start.9 = (f32[2,16,1,256]{3,2,1,0:T(1,128)}, f32[2,16,1,256]{3,2,1,0:T(1,128)S(1)}, u32[]{:S(2)}) copy-start(f32[2,16,1,256]{3,2,1,0:T(1,128)S(1)} %collective-permute-done.11.z_high_ref) | copy-start | bytes 98308
  187.9 0.7 copy-start.4
  187.9 0.8 copy-start.5

commit v2 on v1

--- a/solution.py
+++ b/solution.py
@@ -71,17 +71,23 @@
                 y_last_ref[c] = value
 
 
-def factor_kernel(lam_ref, phase_ref, labels_ref, factor_ref, w_ref, *edge_refs, rows):
-    step = pl.program_id(0)
+def step_factor(labels, phase):
+    rate = jnp.where(labels == 1, 0.3, 0.02)
+    rate = jnp.where(labels == 2, 0.6, rate)
+    rate = jnp.where(labels == 3, 1.2, rate).astype(jnp.float32)
+    decay = jnp.exp(-rate)
+    return decay * jnp.cos(phase), decay * jnp.sin(phase)
+
+
+def halo_w(halo):
+    f_real, f_imag = step_factor(halo[3], halo[2])
+    lam_real, lam_imag = halo[0], halo[1]
+    return jnp.stack([f_real * lam_real - f_imag * lam_imag, f_real * lam_imag + f_imag * lam_real])
+
+
+def factor_kernel(lam_ref, phase_ref, labels_ref, factor_ref, w_ref, *, rows):
     for r in range(rows):
-        labels = labels_ref[r]
-        rate = jnp.where(labels == 1, 0.3, 0.02)
-        rate = jnp.where(labels == 2, 0.6, rate)
-        rate = jnp.where(labels == 3, 1.2, rate).astype(jnp.float32)
-        decay = jnp.exp(-rate)
-        phase = phase_ref[r]
-        f_real = decay * jnp.cos(phase)
-        f_imag = decay * jnp.sin(phase)
+        f_real, f_imag = step_factor(labels_ref[r], phase_ref[r])
         lam_real = lam_ref[0, r]
         lam_imag = lam_ref[1, r]
         w_real = f_real * lam_real - f_imag * lam_imag
@@ -90,7 +96,6 @@
         factor_ref[1, r] = f_imag
         w_ref[0, r] = w_real
         w_ref[1, r] = w_imag
-        write_edges(step, rows, r, [w_real, w_imag], *edge_refs)
 
 
 def edge_outputs(comps, length_y, length_z, length_x, rows):
@@ -163,7 +168,11 @@
         count = lax.axis_size(axis)
         up = [(i, (i + 1) % count) for i in range(count)]
         down = [(j, i) for i, j in up]
-        results.extend([lax.ppermute(last, axis, up), lax.ppermute(first, axis, down)])
+        if count == 2:
+            both = lax.ppermute(jnp.stack([last, first]), axis, up)
+            results.extend([both[0], both[1]])
+        else:
+            results.extend([lax.ppermute(last, axis, up), lax.ppermute(first, axis, down)])
     return results
 
 
@@ -186,15 +195,17 @@
     whole = lambda shape: pl.BlockSpec(shape, lambda i: (0,) * len(shape))
     zspec = lambda comps: pl.BlockSpec((comps, rows, 1, length_x), lambda i: (0, i, 0, 0))
     edge_shapes, edge_specs = edge_outputs(2, length_y, length_z, length_x, rows)
-    factor, w_first, *w_edges = pl.pallas_call(
+    halos = send_edges(*input_edges(
+        [mag_middle, mag_start, adjoint_end, phase[None], labels[None].astype(jnp.float32)]))
+    mag_halos = [h[:4] for h in halos]
+    w_halos = [halo_w(h[4:]) for h in halos]
+    factor, w_first = pl.pallas_call(
         functools.partial(factor_kernel, rows=rows),
         grid=grid,
         in_specs=[cur, cur_plane, cur_plane],
-        out_specs=[cur, cur] + edge_specs,
-        out_shape=[pair, pair] + edge_shapes,
+        out_specs=[cur, cur],
+        out_shape=[pair, pair],
     )(adjoint_end, phase, labels)
-    mag_halos = send_edges(*input_edges([mag_middle, mag_start]))
-    w_halos = send_edges(*w_edges)
     phase_grad, w_second, *w2_edges = pl.pallas_call(
         functools.partial(first_kernel, rows=rows),
         grid=grid,

time: 200 us -> 205 us (1.025)
  local copies, waits for them, and re-layouts: 18.2 us -> 29.8 us
  waiting for transfers between devices: 102 us -> 92.4 us
  other arithmetic: 0.31 us -> 6.49 us
  starting transfers between devices: 27.2 us -> 23.6 us
    ppermute x6 -> x2, waiting for transfers between devices: 49.2 us -> 32.5 us  [send_edges(): lax.ppermute(last, axis, up)]
    ppermute x0 -> x2, waiting for transfers between devices: none -> 13 us  [send_edges(): both = lax.ppermute(jnp.stack([last, first]), axis, up)]
    unnamed x32 -> x20, local copies, waits for them, and re-layouts: 1.94 us -> 12.3 us
    ppermute x6 -> x2, starting transfers between devices: 11.3 us -> 3.48 us  [send_edges(): lax.ppermute(first, axis, down)]
    ppermute x6 -> x2, waiting for transfers between devices: 6.05 us -> 0.01 us  [send_edges(): lax.ppermute(first, axis, down)]
    all_to_all x2, starting transfers between devices: 11.1 us -> 17 us  [dipole_adjoint(): spec = lax.all_to_all(spec, ('gy', 'gz'), 0, 0, tiled=True)]
    ppermute x6 -> x2, starting transfers between devices: 4.76 us -> 0.01 us  [send_edges(): lax.ppermute(last, axis, up)]
    ppermute x0 -> x2, starting transfers between devices: none -> 3.09 us  [send_edges(): both = lax.ppermute(jnp.stack([last, first]), axis, up)]
  transfers between devices with their start and end apart: 14 -> 8, of which waited for: 8 -> 3; matrix products, arithmetic and copies ran while one was open for 1% -> 4% of each run, Pallas kernels for 9% -> 9%
where the time goes in v2:
time: 205 us; the launch traced here: 204 us
  waiting for transfers between devices  92.4 us (45%)
  Pallas kernels  33.4 us (16%)
  local copies, waits for them, and re-layouts  29.8 us (15%)
  starting transfers between devices  23.6 us (12%)
  matrix products  17.4 us (8%)
  other arithmetic  6.49 us (3%)
    all_to_all x2, waiting for transfers between devices, dipole_adjoint(): spec = lax.all_to_all(spec, ('gy', 'gz'), 0, 0, tiled=True)  47 us
    ppermute x2, waiting for transfers between devices, send_edges(): lax.ppermute(last, axis, up)  32.5 us
    dot_general x6, matrix products, along(): return jnp.einsum(spec, table, values, precision=lax.Precision.HIGH)  17.4 us
    all_to_all x2, starting transfers between devices, dipole_adjoint(): spec = lax.all_to_all(spec, ('gy', 'gz'), 0, 0, tiled=True)  17 us
    pallas_call x1, Pallas kernels, backward_sections(): pl.pallas_call(functools.partial(first_kernel, rows=rows), grid=grid, in_...  14.8 us
    ppermute x2, waiting for transfers between devices, send_edges(): both = lax.ppermute(jnp.stack([last, first]), axis, up)  13 us
    unnamed x20, local copies, waits for them, and re-layouts  12.3 us
    pallas_call x1, Pallas kernels, backward_sections(): pl.pallas_call(functools.partial(factor_kernel, rows=rows), grid=grid, in...  11.9 us
  transfers between devices with their start and end apart: 8, of which 3 were waited for; matrix products, arithmetic and copies ran while one was open for 4% of the time, Pallas kernels for 9%

profile of v2, /device:TPU:16, one launch (start us, length us, event | category | flops | bytes accessed | tf_op | source)
XLA Modules:
  0.0 204.0 jit_solution(7127889894569084710)
XLA Ops:
  0.6 1.7 convert_bitcast_fusion
  2.4 1.8 bitcast_dynamic-update-slice_fusion.2
  4.2 1.9 bitcast_dynamic-update-slice_fusion.1
  6.1 1.9 bitcast_dynamic-update-slice_fusion
  7.9 1.7 fusion.36
  9.6 0.7 fusion.35
  10.3 0.8 collective-permute-start.1
  11.2 1.1 constant_dynamic-update-slice_fusion.4
  12.3 1.1 constant_dynamic-update-slice_fusion.3
  13.3 1.1 constant_dynamic-update-slice_fusion.2
  14.4 1.0 constant_dynamic-update-slice_fusion.1
  15.5 0.3 pad_maximum_fusion
  15.7 1.6 collective-permute-start.2
  17.3 11.9 %shard_map.68 = (f32[2,16,128,256]{3,2,1,0:T(8,128)}, f32[2,16,128,256]{3,2,1,0:T(8,128)}) custom-call(f32[2,16,128,256]{3,2,1,0:T(8,128)} %lam_ref.1, f32[16,128,256]{2,1,0:T(8,128)} %phase_ref.1, s32[16,128,256]{2,1,0:T(8,128)} %labels_ref.1), custom_call_target="tpu_custom_call" | custom-call | tf_op jit(solution)/shard_map/pallas_call | solution.py:202
  29.2 1.1 subtract_bitcast_fusion
  30.3 0.7 pad_maximum_fusion.4
  31.0 0.7 slice_bitcast_fusion.4
  31.6 0.5 multiply_subtract_fusion
  32.2 0.7 pad_maximum_fusion.2.refs_15_
  32.9 0.5 multiply_subtract_fusion.1
  33.5 0.7 pad_maximum_fusion.1.refs_14_
  34.2 0.9 slice.214.refs_10_
  35.1 0.8 slice.217.refs_11_
  35.9 14.8 %shard_map.69 = (f32[16,128,256]{2,1,0:T(8,128)}, f32[2,16,128,256]{3,2,1,0:T(8,128)}, f32[2,128,256]{2,1,0:T(8,128)}, f32[2,128,256]{2,1,0:T(8,128)}, f32[2,16,...) custom-call(f32[2,16,128,256]{3,2,1,0:T(8,128)} %refs_2_.1, f32[2,16,128,256]{3,2,1,0:T(8,128)} %refs_2_.1, ...), custom_call_target="tpu_custom_call" | custom-call | tf_op jit(solution)/shard_map/pallas_call | solution.py:209
  50.7 3.7 %convolution_bitcast_fusion = f32[32,8,16,128]{3,1,0,2:T(8,128)S(1)} fusion(f32[16,128,256]{2,1,0:T(8,128)} %get-tuple-element.17), kind=kOutput, calls=%fused_computation.14 | convolution fusion | flops 806289408 | bytes 4194304 | tf_op jit(solution)/shard_map/kn,yzn->kyz/dot_general | solution.py:31
  54.4 2.5 %copy.27 = f32[32,8,16,128]{3,2,1,0:T(8,128)} copy(f32[32,8,16,128]{3,1,0,2:T(8,128)S(1)} %convolution_bitcast_fusion) | data formatting | bytes 4194304 | tf_op jit(solution)/shard_map/reshape | solution.py:245
  56.9 11.7 %all-to-all-start = ((f32[32,8,16,128]{3,2,1,0:T(8,128)}), f32[32,8,16,128]{3,2,1,0:T(8,128)S(1)}, u32[]{:S(2)}, u32[]{:S(2)}) async-start(f32[32,8,16,128]{3,2,1,0:T(8,128)} %copy.27), calls=%async_computation | async-start | bytes 4194304 | tf_op jit(solution)/shard_map/all_to_all | solution.py:246
  68.7 0.1 broadcast_add_fusion
  68.8 47.0 %all-to-all-done = f32[32,8,16,128]{3,2,1,0:T(8,128)S(1)} async-done(((f32[32,8,16,128]{3,2,1,0:T(8,128)}), f32[32,8,16,128]{3,2,1,0:T(8,128)S(1)}, u32[]{:S(2)}, u32[]{:S(2)}) %all-to-all-start) | async-done | bytes 2097184 | tf_op jit(solution)/shard_map/all_to_all | solution.py:246
  115.8 2.9 %copy.28 = f32[8,16,16,2,128]{4,3,2,1,0:T(2,128)} copy(f32[8,16,16,2,128]{4,2,0,3,1:T(8,128)S(1)} %bitcast.96) | data formatting | bytes 4194304 | tf_op jit(solution)/shard_map/transpose | solution.py:248
  118.7 2.9 %reshape.496 = f32[8,256,256]{2,1,0:T(8,128)S(1)} reshape(f32[8,16,16,2,128]{4,3,2,1,0:T(2,128)} %copy.28) | data formatting | bytes 4194304 | tf_op jit(solution)/shard_map/reshape | solution.py:248
  121.6 2.1 %fusion.29 = f32[8,256,256]{1,2,0:T(8,128)S(1)} fusion(f32[8,256,256]{2,1,0:T(8,128)S(1)} %reshape.496), kind=kOutput, calls=%fused_computation.42 | convolution fusion | flops 806289408 | bytes 4194304 | tf_op jit(solution)/shard_map/kz,xyz->xyk/dot_general | solution.py:31
  123.7 2.1 %fusion.27 = f32[8,256,256]{2,1,0:T(8,128)S(1)} fusion(f32[8,256,256]{1,2,0:T(8,128)S(1)} %fusion.29), kind=kOutput, calls=%fused_computation.40 | convolution fusion | flops 806289408 | bytes 4194304 | tf_op jit(solution)/shard_map/ky,xyz->xkz/dot_general | solution.py:31
  125.8 2.6 %fusion.9 = f32[8,256,256]{2,1,0:T(8,128)S(1)} fusion(f32[8,256,256]{2,1,0:T(8,128)S(1)} %fusion.27, f32[256]{0:T(256)S(1)} %fusion.45, s32[8]{0:T(128)S(1)} %fusion.44, s32[256,256]{0,1:T(8,128)S(1)} %broadcast_add_fusion), kind=kOutput, calls=%fused_computation.12 | convolution fusion | flops 810483712 | bytes 4457504 | tf_op jit(solution)/shard_map/ky,xyz->xkz/dot_general | solution.py:31
  128.4 2.7 %fusion.5 = f32[8,256,256]{2,1,0:T(8,128)S(1)} fusion(f32[8,256,256]{2,1,0:T(8,128)S(1)} %fusion.9), kind=kOutput, calls=%fused_computation.7 | convolution fusion | flops 806289408 | bytes 4194304 | tf_op jit(solution)/shard_map/kz,xyz->xyk/dot_general | solution.py:31
  131.1 2.1 %reshape.497 = f32[8,16,16,2,128]{4,3,2,1,0:T(2,128)} reshape(f32[8,256,256]{2,1,0:T(8,128)S(1)} %fusion.5) | data formatting | bytes 4194304 | tf_op jit(solution)/shard_map/reshape | solution.py:259
  133.2 3.2 %copy.31 = f32[8,16,16,2,128]{4,2,0,3,1:T(8,128)} copy(f32[8,16,16,2,128]{4,3,2,1,0:T(2,128)} %reshape.497) | data formatting | bytes 4194304 | tf_op jit(solution)/shard_map/reshape | solution.py:259
  136.4 5.3 %all-to-all-start.1 = ((f32[32,8,16,128]{3,2,1,0:T(8,128)}), f32[32,8,16,128]{3,2,1,0:T(8,128)S(1)}, u32[]{:S(2)}, u32[]{:S(2)}) async-start(f32[32,8,16,128]{3,2,1,0:T(8,128)} %bitcast.95), calls=%async_computation.1 | async-start | bytes 4194304 | tf_op jit(solution)/shard_map/all_to_all | solution.py:261
  141.8 0.1 pad_maximum_fusion.3
  141.8 1.5 collective-permute-start.5
  143.4 2.6 %collective-permute-start.4 = (f32[2,128,256]{2,1,0:T(8,128)S(1)}, f32[2,128,256]{2,1,0:T(8,128)S(1)}, u32[]{:S(2)}, u32[]{:S(2)}) collective-permute-start(f32[2,128,256]{2,1,0:T(8,128)S(1)} %copy-done.4), channel_id=1, source_target_pairs={{2,0},{4,2},{6,4},{8,6},{10,8},{12,10},{14,12},{16,14},{18,16},{20... | collective-permute-start | bytes 786440 | tf_op jit(solution)/shard_map/ppermute | solution.py:175
  146.0 13.0 %collective-permute-done.5 = f32[2,2,16,1,256]{4,3,2,1,0:T(1,128)S(1)} collective-permute-done((f32[2,2,16,1,256]{4,3,2,1,0:T(1,128)S(1)}, f32[2,2,16,1,256]{4,3,2,1,0:T(1,128)S(1)}, u32[]{:S(2)}, u32[]{:S(2)}) %collective-permute-start.5) | collective-permute-done | bytes 65568 | tf_op jit(solution)/shard_map/ppermute | solution.py:172
  159.0 0.6 slice_bitcast_fusion.6
  159.6 32.5 %collective-permute-done.3.y_low_ref = f32[2,128,256]{2,1,0:T(8,128)S(1)} collective-permute-done((f32[2,128,256]{2,1,0:T(8,128)S(1)}, f32[2,128,256]{2,1,0:T(8,128)S(1)}, u32[]{:S(2)}, u32[]{:S(2)}) %collective-permute-start.3) | collective-permute-done | bytes 262176 | tf_op jit(solution)/shard_map/ppermute | solution.py:175
  192.1 0.7 copy-done
  192.8 0.1 copy-done.1
  192.9 6.8 %shard_map.70 = f32[2,16,128,256]{3,2,1,0:T(8,128)} custom-call(f32[2,16,128,256]{3,2,1,0:T(8,128)} %get-tuple-element.12.w_ref.w_prev.w_next, f32[2,16,128,256]{3,2,1,0:T(8,128)} %get-tuple-element.12.w_ref.w_prev.w_next, f32[2,16,128,256]{3,2,1,0:T(8,128)} %get-tuple-element.12.w_ref.w_prev.w_next, f32[2,128,256]{2,1,0:T(8,128)} %copy-done, ...), custom_call_target="tpu_custom_call" | custom-call | tf_op jit(solution)/shard_map/pallas_call | solution.py:221
  199.6 4.3 %fusion.11 = f32[16,128,256]{2,1,0:T(8,128)} fusion(f32[256,16,128]{2,1,0:T(8,128)S(1)} %bitcast.94), kind=kOutput, calls=%fused_computation.13 | convolution fusion | flops 806813696 | bytes 4194304 | tf_op jit(solution)/shard_map/kn,nyz->yzk/dot_general | solution.py:31
  (21 shorter events, 0.1 us)
Async XLA Ops:
  10.3 21.3 %collective-permute-start.1 = (f32[8,128,256]{2,1,0:T(8,128)}, f32[8,128,256]{2,1,0:T(8,128)S(1)}, u32[]{:S(2)}, u32[]{:S(2)}) collective-permute-start(f32[8,128,256]{2,1,0:T(8,128)} %get-tuple-element.34), channel_id=1, source_target_pairs={{2,0},{4,2},{6,4},{8,6},{10,8},{12,10},{14,12},{16,14},{18,16},{20... | collective-permute-start | bytes 3145736 | tf_op jit(solution)/shard_map/ppermute | solution.py:175
  15.7 13.4 %collective-permute-start.2 = (f32[2,8,16,1,256]{4,3,2,1,0:T(1,128)S(1)}, f32[2,8,16,1,256]{4,3,2,1,0:T(1,128)S(1)}, u32[]{:S(2)}, u32[]{:S(2)}) collective-permute-start(f32[2,8,16,1,256]{4,3,2,1,0:T(1,128)S(1)} %pad_maximum_fusion), channel_id=1, source_target_pairs={{0,1},{1,0},{2,3},{3,2},{4,5},{5,4},{6,7},{7,6},{8,9},{9,8},{10,11... | collective-permute-start | bytes 786440 | tf_op jit(solution)/shard_map/ppermute | solution.py:172
  17.3 15.6 %collective-permute-start = (f32[8,128,256]{2,1,0:T(8,128)}, f32[8,128,256]{2,1,0:T(8,128)S(1)}, u32[]{:S(2)}, u32[]{:S(2)}) collective-permute-start(f32[8,128,256]{2,1,0:T(8,128)} %get-tuple-element.35), channel_id=1, source_target_pairs={{0,2},{2,4},{4,6},{6,8},{8,10},{10,12},{12,14},{14,16},{16,18},{18... | collective-permute-start | bytes 3145736 | tf_op jit(solution)/shard_map/ppermute | solution.py:175
  56.9 58.8 %all-to-all-start = ((f32[32,8,16,128]{3,2,1,0:T(8,128)}), f32[32,8,16,128]{3,2,1,0:T(8,128)S(1)}, u32[]{:S(2)}, u32[]{:S(2)}) async-start(f32[32,8,16,128]{3,2,1,0:T(8,128)} %copy.27), calls=%async_computation | async-start | bytes 4194304 | tf_op jit(solution)/shard_map/all_to_all | solution.py:246
  136.4 5.3 %copy-start.2 = (f32[2,16,1,256]{3,2,1,0:T(1,128)S(1)}, f32[2,16,1,256]{3,2,1,0:T(1,128)}, u32[]{:S(2)}) copy-start(f32[2,16,1,256]{3,2,1,0:T(1,128)} %get-tuple-element.16) | copy-start | bytes 98308
  136.4 5.3 %copy-start.3 = (f32[2,16,1,256]{3,2,1,0:T(1,128)S(1)}, f32[2,16,1,256]{3,2,1,0:T(1,128)}, u32[]{:S(2)}) copy-start(f32[2,16,1,256]{3,2,1,0:T(1,128)} %get-tuple-element.15) | copy-start | bytes 98308
  136.4 6.9 %copy-start.5 = (f32[2,128,256]{2,1,0:T(8,128)S(1)}, f32[2,128,256]{2,1,0:T(8,128)}, u32[]{:S(2)}) copy-start(f32[2,128,256]{2,1,0:T(8,128)} %get-tuple-element.13) | copy-start | bytes 786436
  136.4 6.9 %copy-start.4 = (f32[2,128,256]{2,1,0:T(8,128)S(1)}, f32[2,128,256]{2,1,0:T(8,128)}, u32[]{:S(2)}) copy-start(f32[2,128,256]{2,1,0:T(8,128)} %get-tuple-element.14) | copy-start | bytes 786436
  136.4 63.2 %all-to-all-start.1 = ((f32[32,8,16,128]{3,2,1,0:T(8,128)}), f32[32,8,16,128]{3,2,1,0:T(8,128)S(1)}, u32[]{:S(2)}, u32[]{:S(2)}) async-start(f32[32,8,16,128]{3,2,1,0:T(8,128)} %bitcast.95), calls=%async_computation.1 | async-start | bytes 4194304 | tf_op jit(solution)/shard_map/all_to_all | solution.py:261
  141.8 17.2 %collective-permute-start.5 = (f32[2,2,16,1,256]{4,3,2,1,0:T(1,128)S(1)}, f32[2,2,16,1,256]{4,3,2,1,0:T(1,128)S(1)}, u32[]{:S(2)}, u32[]{:S(2)}) collective-permute-start(f32[2,2,16,1,256]{4,3,2,1,0:T(1,128)S(1)} %pad_maximum_fusion.3), channel_id=1, source_target_pairs={{0,1},{1,0},{2,3},{3,2},{4,5},{5,4},{6,7},{7,6},{8,9},{9,8},{10,11... | collective-permute-start | bytes 196616 | tf_op jit(solution)/shard_map/ppermute | solution.py:172
  143.4 48.7 %collective-permute-start.3 = (f32[2,128,256]{2,1,0:T(8,128)S(1)}, f32[2,128,256]{2,1,0:T(8,128)S(1)}, u32[]{:S(2)}, u32[]{:S(2)}) collective-permute-start(f32[2,128,256]{2,1,0:T(8,128)S(1)} %copy-done.5), channel_id=1, source_target_pairs={{0,2},{2,4},{4,6},{6,8},{8,10},{10,12},{12,14},{14,16},{16,18},{18... | collective-permute-start | bytes 786440 | tf_op jit(solution)/shard_map/ppermute | solution.py:175
  143.4 48.7 %collective-permute-start.4 = (f32[2,128,256]{2,1,0:T(8,128)S(1)}, f32[2,128,256]{2,1,0:T(8,128)S(1)}, u32[]{:S(2)}, u32[]{:S(2)}) collective-permute-start(f32[2,128,256]{2,1,0:T(8,128)S(1)} %copy-done.4), channel_id=1, source_target_pairs={{2,0},{4,2},{6,4},{8,6},{10,8},{12,10},{14,12},{16,14},{18,16},{20... | collective-permute-start | bytes 786440 | tf_op jit(solution)/shard_map/ppermute | solution.py:175
  192.1 0.7 copy-start
  192.1 0.8 copy-start.1

commit v3 on v2

--- a/solution.py
+++ b/solution.py
@@ -79,23 +79,53 @@
     return decay * jnp.cos(phase), decay * jnp.sin(phase)
 
 
-def halo_w(halo):
-    f_real, f_imag = step_factor(halo[3], halo[2])
-    lam_real, lam_imag = halo[0], halo[1]
-    return jnp.stack([f_real * lam_real - f_imag * lam_imag, f_real * lam_imag + f_imag * lam_real])
+def first_w(lam_real, lam_imag, labels, phase):
+    f_real, f_imag = step_factor(labels, phase)
+    return (f_real * lam_real - f_imag * lam_imag, f_real * lam_imag + f_imag * lam_real), (f_real, f_imag)
 
 
 def factor_kernel(lam_ref, phase_ref, labels_ref, factor_ref, w_ref, *, rows):
     for r in range(rows):
-        f_real, f_imag = step_factor(labels_ref[r], phase_ref[r])
-        lam_real = lam_ref[0, r]
-        lam_imag = lam_ref[1, r]
-        w_real = f_real * lam_real - f_imag * lam_imag
-        w_imag = f_real * lam_imag + f_imag * lam_real
+        (w_real, w_imag), (f_real, f_imag) = first_w(lam_ref[0, r], lam_ref[1, r], labels_ref[r], phase_ref[r])
         factor_ref[0, r] = f_real
         factor_ref[1, r] = f_imag
         w_ref[0, r] = w_real
         w_ref[1, r] = w_imag
+
+
+def edges_kernel(*refs, rows):
+    (mm_y0, mm_y1, mm_z0, mm_z1, ms_y0, ms_y1, ms_z0, ms_z1, lam_y0, lam_y1, lam_z0, lam_z1,
+     ph_y0, ph_y1, ph_z0, ph_z1, lb_y0, lb_y1, lb_z0, lb_z1,
+     y_first_ref, y_last_ref, z_first_ref, z_last_ref) = refs
+
+    @pl.when(pl.program_id(0) == 0)
+    def _():
+        for out_ref, m1, m2, lam, ph, lb in ((y_first_ref, mm_y0, ms_y0, lam_y0, ph_y0, lb_y0),
+                                           (y_last_ref, mm_y1, ms_y1, lam_y1, ph_y1, lb_y1)):
+            (w_real, w_imag), _ = first_w(lam[0, 0], lam[1, 0], lb[0], ph[0])
+            planes = [m1[0, 0], m1[1, 0], m2[0, 0], m2[1, 0], w_real, w_imag]
+            for c, value in enumerate(planes):
+                out_ref[c] = value
+
+    for r in range(rows):
+        for out_ref, m1, m2, lam, ph, lb, at in ((z_first_ref, mm_z0, ms_z0, lam_z0, ph_z0, lb_z0, 0),
+                                               (z_last_ref, mm_z1, ms_z1, lam_z1, ph_z1, lb_z1, 7)):
+            (w_real, w_imag), _ = first_w(lam[0, r], lam[1, r], lb[r], ph[r])
+            tiles = [m1[0, r], m1[1, r], m2[0, r], m2[1, r], w_real, w_imag]
+            for c, value in enumerate(tiles):
+                out_ref[c, r] = value[at:at + 1]
+
+
+def edge_specs_of(ndim, length_y, length_z, length_x, rows):
+    lead = (2,) if ndim == 4 else ()
+    zero = (0,) * len(lead)
+    tiles = length_z // 8
+    return [
+        pl.BlockSpec(lead + (1, length_z, length_x), lambda i: zero + (0, 0, 0)),
+        pl.BlockSpec(lead + (1, length_z, length_x), lambda i: zero + (length_y - 1, 0, 0)),
+        pl.BlockSpec(lead + (rows, 8, length_x), lambda i: zero + (i, 0, 0)),
+        pl.BlockSpec(lead + (rows, 8, length_x), lambda i: zero + (i, tiles - 1, 0)),
+    ]
 
 
 def edge_outputs(comps, length_y, length_z, length_x, rows):
@@ -108,20 +138,17 @@
 
 def first_kernel(*refs, rows):
     (mm_ref, mm_prev, mm_next, ms_ref, ms_prev, ms_next, w_ref, w_prev, w_next,
-     factor_ref, *halo_refs) = refs[:18]
-    pg_ref, w2_ref = refs[18:20]
+     factor_ref, y_low_ref, y_high_ref, z_low_ref, z_high_ref, pg_ref, w2_ref) = refs[:16]
     step = pl.program_id(0)
     fields = ((mm_ref, mm_prev, mm_next), (ms_ref, ms_prev, ms_next), (w_ref, w_prev, w_next))
     for r in range(rows):
         new = []
         for f, (cur, prev, nxt) in enumerate(fields):
-            y_low_ref, y_high_ref, z_low_ref, z_high_ref = halo_refs[4 * (f // 2):4 * (f // 2) + 4]
             pair = []
             for comp in range(2):
-                index = 2 * f + comp if f < 2 else comp
-                below, above = neighbour_planes(cur, prev, nxt, y_low_ref, y_high_ref, rows, index, comp, r)
+                below, above = neighbour_planes(cur, prev, nxt, y_low_ref, y_high_ref, rows, 2 * f + comp, comp, r)
                 pair.append(plane_update(cur[comp, r], below, above,
-                                         z_low_ref[index, r], z_high_ref[index, r]))
+                                         z_low_ref[2 * f + comp, r], z_high_ref[2 * f + comp, r]))
             new.append(pair)
         (u1_real, u1_imag), (u2_real, u2_imag), (lam_real, lam_imag) = new
         w_real = w_ref[0, r]
@@ -134,7 +161,7 @@
         pg_ref[r] = grad + (w2_real * u2_imag - w2_imag * u2_real)
         w2_ref[0, r] = w2_real
         w2_ref[1, r] = w2_imag
-        write_edges(step, rows, r, [w2_real, w2_imag], *refs[20:])
+        write_edges(step, rows, r, [w2_real, w2_imag], *refs[16:])
 
 
 def second_kernel(w_ref, w_prev, w_next, y_low_ref, y_high_ref, z_low_ref, z_high_ref, out_ref, *, rows):
@@ -176,14 +203,6 @@
     return results
 
 
-def input_edges(fields):
-    y_first = jnp.concatenate([f[:, 0] for f in fields])
-    y_last = jnp.concatenate([f[:, -1] for f in fields])
-    z_first = jnp.concatenate([f[:, :, 0:1] for f in fields])
-    z_last = jnp.concatenate([f[:, :, -1:] for f in fields])
-    return [y_first, y_last, z_first, z_last]
-
-
 def backward_sections(mag_start, mag_middle, adjoint_end, phase, labels):
     _, length_y, length_z, length_x = mag_start.shape
     rows = block_rows(length_y)
@@ -195,10 +214,16 @@
     whole = lambda shape: pl.BlockSpec(shape, lambda i: (0,) * len(shape))
     zspec = lambda comps: pl.BlockSpec((comps, rows, 1, length_x), lambda i: (0, i, 0, 0))
     edge_shapes, edge_specs = edge_outputs(2, length_y, length_z, length_x, rows)
-    halos = send_edges(*input_edges(
-        [mag_middle, mag_start, adjoint_end, phase[None], labels[None].astype(jnp.float32)]))
-    mag_halos = [h[:4] for h in halos]
-    w_halos = [halo_w(h[4:]) for h in halos]
+    six_shapes, six_specs = edge_outputs(6, length_y, length_z, length_x, rows)
+    inputs = (mag_middle, mag_start, adjoint_end, phase, labels)
+    edges = pl.pallas_call(
+        functools.partial(edges_kernel, rows=rows),
+        grid=grid,
+        in_specs=[s for a in inputs for s in edge_specs_of(a.ndim, length_y, length_z, length_x, rows)],
+        out_specs=six_specs,
+        out_shape=six_shapes,
+    )(*[a for a in inputs for _ in range(4)])
+    halos = send_edges(*edges)
     factor, w_first = pl.pallas_call(
         functools.partial(factor_kernel, rows=rows),
         grid=grid,
@@ -211,12 +236,11 @@
         grid=grid,
         in_specs=field_specs(mag_middle.shape, rows) + field_specs(mag_start.shape, rows)
         + field_specs(w_first.shape, rows)
-        + [cur, whole((4, length_z, length_x)), whole((4, length_z, length_x)), zspec(4), zspec(4),
-           whole((2, length_z, length_x)), whole((2, length_z, length_x)), zspec(2), zspec(2)],
+        + [cur, whole((6, length_z, length_x)), whole((6, length_z, length_x)), zspec(6), zspec(6)],
         out_specs=[cur_plane, cur] + edge_specs,
         out_shape=[plane, pair] + edge_shapes,
     )(mag_middle, mag_middle, mag_middle, mag_start, mag_start, mag_start,
-      w_first, w_first, w_first, factor, *mag_halos, *w_halos)
+      w_first, w_first, w_first, factor, *halos)
     halos = send_edges(*w2_edges)
     lam = pl.pallas_call(
         functools.partial(second_kernel, rows=rows),

time: 205 us -> 191 us (0.932)
  local copies, waits for them, and re-layouts: 29.8 us -> 17.1 us
  Pallas kernels: 33.4 us -> 39.6 us
  other arithmetic: 6.49 us -> 1.32 us
    unnamed x20 -> x16, local copies, waits for them, and re-layouts: 12.3 us -> 2.01 us
    pallas_call x0 -> x1, Pallas kernels: none -> 6.26 us  [backward_sections(): pl.pallas_call(functools.partial(edges_kernel, rows=rows), grid=grid, in_...]
    all_to_all x2, starting transfers between devices: 17 us -> 13.3 us  [dipole_adjoint(): spec = lax.all_to_all(spec, ('gy', 'gz'), 0, 0, tiled=True)]
    slice x3 -> x0, local copies, waits for them, and re-layouts: 2.4 us -> none  [backward_sections(): mag_halos = [h[:4] for h in halos]]
    another operation x3 -> x0, other arithmetic: 2.17 us -> none  [halo_w(): jnp.stack([f_real * lam_real - f_imag * lam_imag, f_real * lam_imag + f_i...]
    sub x3 -> x0, other arithmetic: 2.15 us -> none  [halo_w(): f_real * lam_real - f_imag * lam_imag]
  transfers between devices with their start and end apart: 8 -> 8, of which waited for: 3 -> 3; matrix products, arithmetic and copies ran while one was open for 4% -> 1% of each run, Pallas kernels for 9% -> 10%
where the time goes in v3:
time: 191 us; the launch traced here: 190 us
  waiting for transfers between devices  92.4 us (48%)
  Pallas kernels  39.6 us (21%)
  starting transfers between devices  21.7 us (11%)
  matrix products  17.4 us (9%)
  local copies, waits for them, and re-layouts  17.1 us (9%)
    all_to_all x2, waiting for transfers between devices, dipole_adjoint(): spec = lax.all_to_all(spec, ('gy', 'gz'), 0, 0, tiled=True)  47 us
    ppermute x2, waiting for transfers between devices, send_edges(): lax.ppermute(last, axis, up)  32.4 us
    dot_general x6, matrix products, along(): return jnp.einsum(spec, table, values, precision=lax.Precision.HIGH)  17.4 us
    pallas_call x1, Pallas kernels, backward_sections(): pl.pallas_call(functools.partial(first_kernel, rows=rows), grid=grid, in_...  14.8 us
    all_to_all x2, starting transfers between devices, dipole_adjoint(): spec = lax.all_to_all(spec, ('gy', 'gz'), 0, 0, tiled=True)  13.3 us
    ppermute x2, waiting for transfers between devices, send_edges(): both = lax.ppermute(jnp.stack([last, first]), axis, up)  13 us
    pallas_call x1, Pallas kernels, backward_sections(): pl.pallas_call(functools.partial(factor_kernel, rows=rows), grid=grid, in...  11.8 us
    pallas_call x1, Pallas kernels, backward_sections(): pl.pallas_call(functools.partial(second_kernel, rows=rows), grid=grid, in...  6.75 us
  transfers between devices with their start and end apart: 8, of which 3 were waited for; matrix products, arithmetic and copies ran while one was open for 1% of the time, Pallas kernels for 10%

profile of v3, /device:TPU:16, one launch (start us, length us, event | category | flops | bytes accessed | tf_op | source)
XLA Modules:
  0.0 190.4 jit_solution(1289921872428291152)
XLA Ops:
  0.6 6.3 %shard_map.69 = (f32[6,128,256]{2,1,0:T(8,128)}, f32[6,128,256]{2,1,0:T(8,128)}, f32[6,16,1,256]{3,2,1,0:T(1,128)}, f32[6,16,1,256]{3,2,1,0:T(1,128)}) custom-call(f32[2,16,128,256]{3,2,1,0:T(8,128)} %refs_2_.3, f32[2,16,128,256]{3,2,1,0:T(8,128)} %refs_2_.3, f32[2,16,128,256]{3,2,1,0:T(8,128)} %refs_2_.3, f32[2,16,128,256]{3,2,1,0:T(8,128)} %refs_2_.3, ...), custom_call_target="tpu_custom_call" | custom-call | tf_op jit(solution)/shard_map/pallas_call | solution.py:219
  6.9 0.1 collective-permute-start
  7.0 2.6 %collective-permute-start.1 = (f32[6,128,256]{2,1,0:T(8,128)}, f32[6,128,256]{2,1,0:T(8,128)S(1)}, u32[]{:S(2)}, u32[]{:S(2)}) collective-permute-start(f32[6,128,256]{2,1,0:T(8,128)} %get-tuple-element.17), channel_id=1, source_target_pairs={{2,0},{4,2},{6,4},{8,6},{10,8},{12,10},{14,12},{16,14},{18,16},{20... | collective-permute-start | bytes 2359304 | tf_op jit(solution)/shard_map/ppermute | solution.py:202
  9.6 1.1 pad_maximum_fusion
  10.7 1.6 collective-permute-start.2
  12.3 11.8 %shard_map.68 = (f32[2,16,128,256]{3,2,1,0:T(8,128)}, f32[2,16,128,256]{3,2,1,0:T(8,128)}) custom-call(f32[2,16,128,256]{3,2,1,0:T(8,128)} %refs_11_.1, f32[16,128,256]{2,1,0:T(8,128)} %refs_15_.1, s32[16,128,256]{2,1,0:T(8,128)} %refs_19_.1), custom_call_target="tpu_custom_call" | custom-call | tf_op jit(solution)/shard_map/pallas_call | solution.py:227
  24.1 0.0 collective-permute-done.2
  24.1 0.8 slice_bitcast_fusion
  24.9 0.0 collective-permute-done.refs_10_
  24.9 0.0 copy-start
  24.9 0.0 collective-permute-done.1.refs_11_
  24.9 0.0 copy-start.1
  25.0 0.9 copy-done
  25.9 0.2 copy-done.1
  26.1 14.8 %shard_map.70 = (f32[16,128,256]{2,1,0:T(8,128)}, f32[2,16,128,256]{3,2,1,0:T(8,128)}, f32[2,128,256]{2,1,0:T(8,128)}, f32[2,128,256]{2,1,0:T(8,128)}, f32[2,16,...) custom-call(f32[2,16,128,256]{3,2,1,0:T(8,128)} %refs_2_.3, f32[2,16,128,256]{3,2,1,0:T(8,128)} %refs_2_.3, ...), custom_call_target="tpu_custom_call" | custom-call | tf_op jit(solution)/shard_map/pallas_call | solution.py:234
  40.9 3.7 %convolution_bitcast_fusion = f32[32,8,16,128]{3,1,0,2:T(8,128)S(1)} fusion(f32[16,128,256]{2,1,0:T(8,128)} %get-tuple-element.25), kind=kOutput, calls=%fused_computation.13 | convolution fusion | flops 806289408 | bytes 4194304 | tf_op jit(solution)/shard_map/kn,yzn->kyz/dot_general | solution.py:31
  44.6 2.5 %copy.9 = f32[32,8,16,128]{3,2,1,0:T(8,128)} copy(f32[32,8,16,128]{3,1,0,2:T(8,128)S(1)} %convolution_bitcast_fusion) | data formatting | bytes 4194304 | tf_op jit(solution)/shard_map/reshape | solution.py:269
  47.1 8.0 %all-to-all-start = ((f32[32,8,16,128]{3,2,1,0:T(8,128)}), f32[32,8,16,128]{3,2,1,0:T(8,128)S(1)}, u32[]{:S(2)}, u32[]{:S(2)}) async-start(f32[32,8,16,128]{3,2,1,0:T(8,128)} %copy.9), calls=%async_computation | async-start | bytes 4194304 | tf_op jit(solution)/shard_map/all_to_all | solution.py:270
  55.2 0.1 broadcast_add_fusion
  55.3 47.0 %all-to-all-done = f32[32,8,16,128]{3,2,1,0:T(8,128)S(1)} async-done(((f32[32,8,16,128]{3,2,1,0:T(8,128)}), f32[32,8,16,128]{3,2,1,0:T(8,128)S(1)}, u32[]{:S(2)}, u32[]{:S(2)}) %all-to-all-start) | async-done | bytes 2097184 | tf_op jit(solution)/shard_map/all_to_all | solution.py:270
  102.2 2.9 %copy.10 = f32[8,16,16,2,128]{4,3,2,1,0:T(2,128)} copy(f32[8,16,16,2,128]{4,2,0,3,1:T(8,128)S(1)} %bitcast.45) | data formatting | bytes 4194304 | tf_op jit(solution)/shard_map/transpose | solution.py:272
  105.2 2.9 %reshape.89 = f32[8,256,256]{2,1,0:T(8,128)S(1)} reshape(f32[8,16,16,2,128]{4,3,2,1,0:T(2,128)} %copy.10) | data formatting | bytes 4194304 | tf_op jit(solution)/shard_map/reshape | solution.py:272
  108.1 2.1 %fusion.29 = f32[8,256,256]{1,2,0:T(8,128)S(1)} fusion(f32[8,256,256]{2,1,0:T(8,128)S(1)} %reshape.89), kind=kOutput, calls=%fused_computation.32 | convolution fusion | flops 806289408 | bytes 4194304 | tf_op jit(solution)/shard_map/kz,xyz->xyk/dot_general | solution.py:31
  110.2 2.1 %fusion.27 = f32[8,256,256]{2,1,0:T(8,128)S(1)} fusion(f32[8,256,256]{1,2,0:T(8,128)S(1)} %fusion.29), kind=kOutput, calls=%fused_computation.30 | convolution fusion | flops 806289408 | bytes 4194304 | tf_op jit(solution)/shard_map/ky,xyz->xkz/dot_general | solution.py:31
  112.3 2.6 %fusion.9 = f32[8,256,256]{2,1,0:T(8,128)S(1)} fusion(f32[8,256,256]{2,1,0:T(8,128)S(1)} %fusion.27, f32[256]{0:T(256)S(1)} %fusion.37, s32[8]{0:T(128)S(1)} %fusion.36, s32[256,256]{0,1:T(8,128)S(1)} %broadcast_add_fusion), kind=kOutput, calls=%fused_computation.11 | convolution fusion | flops 810483712 | bytes 4457504 | tf_op jit(solution)/shard_map/ky,xyz->xkz/dot_general | solution.py:31
  114.9 2.7 %fusion.5 = f32[8,256,256]{2,1,0:T(8,128)S(1)} fusion(f32[8,256,256]{2,1,0:T(8,128)S(1)} %fusion.9), kind=kOutput, calls=%fused_computation.7 | convolution fusion | flops 806289408 | bytes 4194304 | tf_op jit(solution)/shard_map/kz,xyz->xyk/dot_general | solution.py:31
  117.6 2.1 %reshape.90 = f32[8,16,16,2,128]{4,3,2,1,0:T(2,128)} reshape(f32[8,256,256]{2,1,0:T(8,128)S(1)} %fusion.5) | data formatting | bytes 4194304 | tf_op jit(solution)/shard_map/reshape | solution.py:283
  119.7 3.2 %copy.13 = f32[8,16,16,2,128]{4,2,0,3,1:T(8,128)} copy(f32[8,16,16,2,128]{4,3,2,1,0:T(2,128)} %reshape.90) | data formatting | bytes 4194304 | tf_op jit(solution)/shard_map/reshape | solution.py:283
  122.9 0.0 copy-start.4
  122.9 0.0 copy-start.5
  122.9 5.3 %all-to-all-start.1 = ((f32[32,8,16,128]{3,2,1,0:T(8,128)}), f32[32,8,16,128]{3,2,1,0:T(8,128)S(1)}, u32[]{:S(2)}, u32[]{:S(2)}) async-start(f32[32,8,16,128]{3,2,1,0:T(8,128)} %bitcast.44), calls=%async_computation.1 | async-start | bytes 4194304 | tf_op jit(solution)/shard_map/all_to_all | solution.py:285
  128.2 0.0 copy-done.4
  128.2 0.0 copy-done.5
  128.2 0.1 pad_maximum_fusion.1
  128.3 1.5 collective-permute-start.5
  129.8 0.0 copy-done.7
  129.8 0.0 collective-permute-start.3
  129.8 0.0 copy-done.6
  129.8 2.6 %collective-permute-start.4 = (f32[2,128,256]{2,1,0:T(8,128)S(1)}, f32[2,128,256]{2,1,0:T(8,128)S(1)}, u32[]{:S(2)}, u32[]{:S(2)}) collective-permute-start(f32[2,128,256]{2,1,0:T(8,128)S(1)} %copy-done.6), channel_id=1, source_target_pairs={{2,0},{4,2},{6,4},{8,6},{10,8},{12,10},{14,12},{16,14},{18,16},{20... | collective-permute-start | bytes 786440 | tf_op jit(solution)/shard_map/ppermute | solution.py:202
  132.5 13.0 %collective-permute-done.5 = f32[2,2,16,1,256]{4,3,2,1,0:T(1,128)S(1)} collective-permute-done((f32[2,2,16,1,256]{4,3,2,1,0:T(1,128)S(1)}, f32[2,2,16,1,256]{4,3,2,1,0:T(1,128)S(1)}, u32[]{:S(2)}, u32[]{:S(2)}) %collective-permute-start.5) | collective-permute-done | bytes 65568 | tf_op jit(solution)/shard_map/ppermute | solution.py:199
  145.4 0.6 slice_bitcast_fusion.2
  146.1 32.4 %collective-permute-done.3.y_low_ref = f32[2,128,256]{2,1,0:T(8,128)S(1)} collective-permute-done((f32[2,128,256]{2,1,0:T(8,128)S(1)}, f32[2,128,256]{2,1,0:T(8,128)S(1)}, u32[]{:S(2)}, u32[]{:S(2)}) %collective-permute-start.3) | collective-permute-done | bytes 262176 | tf_op jit(solution)/shard_map/ppermute | solution.py:202
  178.5 0.0 collective-permute-done.4.y_high_ref
  178.5 0.7 copy-done.2
  179.2 0.1 copy-done.3
  179.3 6.8 %shard_map.71 = f32[2,16,128,256]{3,2,1,0:T(8,128)} custom-call(f32[2,16,128,256]{3,2,1,0:T(8,128)} %get-tuple-element.20.w_ref.w_prev.w_next, f32[2,16,128,256]{3,2,1,0:T(8,128)} %get-tuple-element.20.w_ref.w_prev.w_next, f32[2,16,128,256]{3,2,1,0:T(8,128)} %get-tuple-element.20.w_ref.w_prev.w_next, f32[2,128,256]{2,1,0:T(8,128)} %copy-done.2, ...), custom_call_target="tpu_custom_call" | custom-call | tf_op jit(solution)/shard_map/pallas_call | solution.py:245
  186.1 0.0 all-to-all-done.1
  186.1 4.3 %fusion.11 = f32[16,128,256]{2,1,0:T(8,128)} fusion(f32[256,16,128]{2,1,0:T(8,128)S(1)} %bitcast.43), kind=kOutput, calls=%fused_computation.12 | convolution fusion | flops 806813696 | bytes 4194304 | tf_op jit(solution)/shard_map/kn,nyz->yzk/dot_general | solution.py:31
  (7 shorter events, 0.0 us)
Async XLA Ops:
  6.9 18.0 %collective-permute-start = (f32[6,128,256]{2,1,0:T(8,128)}, f32[6,128,256]{2,1,0:T(8,128)S(1)}, u32[]{:S(2)}, u32[]{:S(2)}) collective-permute-start(f32[6,128,256]{2,1,0:T(8,128)} %get-tuple-element.16), channel_id=1, source_target_pairs={{0,2},{2,4},{4,6},{6,8},{8,10},{10,12},{12,14},{14,16},{16,18},{18... | collective-permute-start | bytes 2359304 | tf_op jit(solution)/shard_map/ppermute | solution.py:202
  7.0 18.0 %collective-permute-start.1 = (f32[6,128,256]{2,1,0:T(8,128)}, f32[6,128,256]{2,1,0:T(8,128)S(1)}, u32[]{:S(2)}, u32[]{:S(2)}) collective-permute-start(f32[6,128,256]{2,1,0:T(8,128)} %get-tuple-element.17), channel_id=1, source_target_pairs={{2,0},{4,2},{6,4},{8,6},{10,8},{12,10},{14,12},{16,14},{18,16},{20... | collective-permute-start | bytes 2359304 | tf_op jit(solution)/shard_map/ppermute | solution.py:202
  10.7 13.4 %collective-permute-start.2 = (f32[2,6,16,1,256]{4,3,2,1,0:T(1,128)S(1)}, f32[2,6,16,1,256]{4,3,2,1,0:T(1,128)S(1)}, u32[]{:S(2)}, u32[]{:S(2)}) collective-permute-start(f32[2,6,16,1,256]{4,3,2,1,0:T(1,128)S(1)} %pad_maximum_fusion), channel_id=1, source_target_pairs={{0,1},{1,0},{2,3},{3,2},{4,5},{5,4},{6,7},{7,6},{8,9},{9,8},{10,11... | collective-permute-start | bytes 589832 | tf_op jit(solution)/shard_map/ppermute | solution.py:199
  24.9 1.0 copy-start
  24.9 1.2 copy-start.1
  47.1 55.1 %all-to-all-start = ((f32[32,8,16,128]{3,2,1,0:T(8,128)}), f32[32,8,16,128]{3,2,1,0:T(8,128)S(1)}, u32[]{:S(2)}, u32[]{:S(2)}) async-start(f32[32,8,16,128]{3,2,1,0:T(8,128)} %copy.9), calls=%async_computation | async-start | bytes 4194304 | tf_op jit(solution)/shard_map/all_to_all | solution.py:270
  122.9 5.3 %copy-start.4 = (f32[2,16,1,256]{3,2,1,0:T(1,128)S(1)}, f32[2,16,1,256]{3,2,1,0:T(1,128)}, u32[]{:S(2)}) copy-start(f32[2,16,1,256]{3,2,1,0:T(1,128)} %get-tuple-element.24) | copy-start | bytes 98308
  122.9 5.3 %copy-start.5 = (f32[2,16,1,256]{3,2,1,0:T(1,128)S(1)}, f32[2,16,1,256]{3,2,1,0:T(1,128)}, u32[]{:S(2)}) copy-start(f32[2,16,1,256]{3,2,1,0:T(1,128)} %get-tuple-element.23) | copy-start | bytes 98308
  122.9 6.9 %copy-start.7 = (f32[2,128,256]{2,1,0:T(8,128)S(1)}, f32[2,128,256]{2,1,0:T(8,128)}, u32[]{:S(2)}) copy-start(f32[2,128,256]{2,1,0:T(8,128)} %get-tuple-element.21) | copy-start | bytes 786436
  122.9 6.9 %copy-start.6 = (f32[2,128,256]{2,1,0:T(8,128)S(1)}, f32[2,128,256]{2,1,0:T(8,128)}, u32[]{:S(2)}) copy-start(f32[2,128,256]{2,1,0:T(8,128)} %get-tuple-element.22) | copy-start | bytes 786436
  122.9 63.2 %all-to-all-start.1 = ((f32[32,8,16,128]{3,2,1,0:T(8,128)}), f32[32,8,16,128]{3,2,1,0:T(8,128)S(1)}, u32[]{:S(2)}, u32[]{:S(2)}) async-start(f32[32,8,16,128]{3,2,1,0:T(8,128)} %bitcast.44), calls=%async_computation.1 | async-start | bytes 4194304 | tf_op jit(solution)/shard_map/all_to_all | solution.py:285
  128.3 17.2 %collective-permute-start.5 = (f32[2,2,16,1,256]{4,3,2,1,0:T(1,128)S(1)}, f32[2,2,16,1,256]{4,3,2,1,0:T(1,128)S(1)}, u32[]{:S(2)}, u32[]{:S(2)}) collective-permute-start(f32[2,2,16,1,256]{4,3,2,1,0:T(1,128)S(1)} %pad_maximum_fusion.1), channel_id=1, source_target_pairs={{0,1},{1,0},{2,3},{3,2},{4,5},{5,4},{6,7},{7,6},{8,9},{9,8},{10,11... | collective-permute-start | bytes 196616 | tf_op jit(solution)/shard_map/ppermute | solution.py:199
  129.8 48.7 %collective-permute-start.3 = (f32[2,128,256]{2,1,0:T(8,128)S(1)}, f32[2,128,256]{2,1,0:T(8,128)S(1)}, u32[]{:S(2)}, u32[]{:S(2)}) collective-permute-start(f32[2,128,256]{2,1,0:T(8,128)S(1)} %copy-done.7), channel_id=1, source_target_pairs={{0,2},{2,4},{4,6},{6,8},{8,10},{10,12},{12,14},{14,16},{16,18},{18... | collective-permute-start | bytes 786440 | tf_op jit(solution)/shard_map/ppermute | solution.py:202
  129.8 48.7 %collective-permute-start.4 = (f32[2,128,256]{2,1,0:T(8,128)S(1)}, f32[2,128,256]{2,1,0:T(8,128)S(1)}, u32[]{:S(2)}, u32[]{:S(2)}) collective-permute-start(f32[2,128,256]{2,1,0:T(8,128)S(1)} %copy-done.6), channel_id=1, source_target_pairs={{2,0},{4,2},{6,4},{8,6},{10,8},{12,10},{14,12},{16,14},{18,16},{20... | collective-permute-start | bytes 786440 | tf_op jit(solution)/shard_map/ppermute | solution.py:202
  178.5 0.7 copy-start.2
  178.5 0.8 copy-start.3

commit v4 on v3

--- a/solution.py
+++ b/solution.py
@@ -173,7 +173,7 @@
 
 
 def block_rows(length_y):
-    rows = 4
+    rows = 8
     while length_y % rows:
         rows //= 2
     return rows

time: 191 us -> 190 us (level)
  no operation moved by 1% of the time
where the time goes in v4:
time: 190 us; the launch traced here: 189 us
  waiting for transfers between devices  92.4 us (49%)
  Pallas kernels  39.4 us (21%)
  starting transfers between devices  20.5 us (11%)
  local copies, waits for them, and re-layouts  17.4 us (9%)
  matrix products  17.4 us (9%)
    all_to_all x2, waiting for transfers between devices, dipole_adjoint(): spec = lax.all_to_all(spec, ('gy', 'gz'), 0, 0, tiled=True)  47 us
    ppermute x2, waiting for transfers between devices, send_edges(): lax.ppermute(last, axis, up)  32.4 us
    dot_general x6, matrix products, along(): return jnp.einsum(spec, table, values, precision=lax.Precision.HIGH)  17.4 us
    pallas_call x1, Pallas kernels, backward_sections(): pl.pallas_call(functools.partial(first_kernel, rows=rows), grid=grid, in_...  14.9 us
    pallas_call x1, Pallas kernels, backward_sections(): pl.pallas_call(functools.partial(factor_kernel, rows=rows), grid=grid, in...  13.1 us
    ppermute x2, waiting for transfers between devices, send_edges(): both = lax.ppermute(jnp.stack([last, first]), axis, up)  13 us
    all_to_all x2, starting transfers between devices, dipole_adjoint(): spec = lax.all_to_all(spec, ('gy', 'gz'), 0, 0, tiled=True)  12 us
    pallas_call x1, Pallas kernels, backward_sections(): pl.pallas_call(functools.partial(second_kernel, rows=rows), grid=grid, in...  5.94 us
  transfers between devices with their start and end apart: 8, of which 3 were waited for; matrix products, arithmetic and copies ran while one was open for 1% of the time, Pallas kernels for 10%

profile of v4, /device:TPU:16, one launch (start us, length us, event | category | flops | bytes accessed | tf_op | source)
XLA Modules:
  0.0 189.2 jit_solution(16859031876329194930)
XLA Ops:
  0.6 5.5 %shard_map.69 = (f32[6,128,256]{2,1,0:T(8,128)}, f32[6,128,256]{2,1,0:T(8,128)}, f32[6,16,1,256]{3,2,1,0:T(1,128)}, f32[6,16,1,256]{3,2,1,0:T(1,128)}) custom-call(f32[2,16,128,256]{3,2,1,0:T(8,128)} %refs_2_.3, f32[2,16,128,256]{3,2,1,0:T(8,128)} %refs_2_.3, f32[2,16,128,256]{3,2,1,0:T(8,128)} %refs_2_.3, f32[2,16,128,256]{3,2,1,0:T(8,128)} %refs_2_.3, ...), custom_call_target="tpu_custom_call" | custom-call | tf_op jit(solution)/shard_map/pallas_call | solution.py:219
  6.1 0.1 collective-permute-start
  6.2 2.6 %collective-permute-start.1 = (f32[6,128,256]{2,1,0:T(8,128)}, f32[6,128,256]{2,1,0:T(8,128)S(1)}, u32[]{:S(2)}, u32[]{:S(2)}) collective-permute-start(f32[6,128,256]{2,1,0:T(8,128)} %get-tuple-element.17), channel_id=1, source_target_pairs={{2,0},{4,2},{6,4},{8,6},{10,8},{12,10},{14,12},{16,14},{18,16},{20... | collective-permute-start | bytes 2359304 | tf_op jit(solution)/shard_map/ppermute | solution.py:202
  8.8 1.1 pad_maximum_fusion
  10.0 1.6 collective-permute-start.2
  11.5 13.1 %shard_map.68 = (f32[2,16,128,256]{3,2,1,0:T(8,128)}, f32[2,16,128,256]{3,2,1,0:T(8,128)}) custom-call(f32[2,16,128,256]{3,2,1,0:T(8,128)} %refs_11_.1, f32[16,128,256]{2,1,0:T(8,128)} %refs_15_.1, s32[16,128,256]{2,1,0:T(8,128)} %refs_19_.1), custom_call_target="tpu_custom_call" | custom-call | tf_op jit(solution)/shard_map/pallas_call | solution.py:227
  24.6 0.0 collective-permute-done.2
  24.6 0.8 slice_bitcast_fusion
  25.4 0.0 collective-permute-done.refs_10_
  25.4 0.0 copy-start
  25.4 0.0 collective-permute-done.1.refs_11_
  25.4 0.0 copy-start.1
  25.4 0.9 copy-done
  26.4 0.2 copy-done.1
  26.6 14.9 %shard_map.70 = (f32[16,128,256]{2,1,0:T(8,128)}, f32[2,16,128,256]{3,2,1,0:T(8,128)}, f32[2,128,256]{2,1,0:T(8,128)}, f32[2,128,256]{2,1,0:T(8,128)}, f32[2,16,...) custom-call(f32[2,16,128,256]{3,2,1,0:T(8,128)} %refs_2_.3, f32[2,16,128,256]{3,2,1,0:T(8,128)} %refs_2_.3, ...), custom_call_target="tpu_custom_call" | custom-call | tf_op jit(solution)/shard_map/pallas_call | solution.py:234
  41.6 3.7 %convolution_bitcast_fusion = f32[32,8,16,128]{3,1,0,2:T(8,128)S(1)} fusion(f32[16,128,256]{2,1,0:T(8,128)} %get-tuple-element.25), kind=kOutput, calls=%fused_computation.13 | convolution fusion | flops 806289408 | bytes 4194304 | tf_op jit(solution)/shard_map/kn,yzn->kyz/dot_general | solution.py:31
  45.2 2.5 %copy.9 = f32[32,8,16,128]{3,2,1,0:T(8,128)} copy(f32[32,8,16,128]{3,1,0,2:T(8,128)S(1)} %convolution_bitcast_fusion) | data formatting | bytes 4194304 | tf_op jit(solution)/shard_map/reshape | solution.py:269
  47.8 6.7 %all-to-all-start = ((f32[32,8,16,128]{3,2,1,0:T(8,128)}), f32[32,8,16,128]{3,2,1,0:T(8,128)S(1)}, u32[]{:S(2)}, u32[]{:S(2)}) async-start(f32[32,8,16,128]{3,2,1,0:T(8,128)} %copy.9), calls=%async_computation | async-start | bytes 4194304 | tf_op jit(solution)/shard_map/all_to_all | solution.py:270
  54.6 0.1 broadcast_add_fusion
  54.7 47.0 %all-to-all-done = f32[32,8,16,128]{3,2,1,0:T(8,128)S(1)} async-done(((f32[32,8,16,128]{3,2,1,0:T(8,128)}), f32[32,8,16,128]{3,2,1,0:T(8,128)S(1)}, u32[]{:S(2)}, u32[]{:S(2)}) %all-to-all-start) | async-done | bytes 2097184 | tf_op jit(solution)/shard_map/all_to_all | solution.py:270
  101.6 2.9 %copy.10 = f32[8,16,16,2,128]{4,3,2,1,0:T(2,128)} copy(f32[8,16,16,2,128]{4,2,0,3,1:T(8,128)S(1)} %bitcast.45) | data formatting | bytes 4194304 | tf_op jit(solution)/shard_map/transpose | solution.py:272
  104.6 3.2 %reshape.89 = f32[8,256,256]{2,1,0:T(8,128)S(1)} reshape(f32[8,16,16,2,128]{4,3,2,1,0:T(2,128)} %copy.10) | data formatting | bytes 4194304 | tf_op jit(solution)/shard_map/reshape | solution.py:272
  107.7 2.1 %fusion.29 = f32[8,256,256]{1,2,0:T(8,128)S(1)} fusion(f32[8,256,256]{2,1,0:T(8,128)S(1)} %reshape.89), kind=kOutput, calls=%fused_computation.32 | convolution fusion | flops 806289408 | bytes 4194304 | tf_op jit(solution)/shard_map/kz,xyz->xyk/dot_general | solution.py:31
  109.8 2.1 %fusion.27 = f32[8,256,256]{2,1,0:T(8,128)S(1)} fusion(f32[8,256,256]{1,2,0:T(8,128)S(1)} %fusion.29), kind=kOutput, calls=%fused_computation.30 | convolution fusion | flops 806289408 | bytes 4194304 | tf_op jit(solution)/shard_map/ky,xyz->xkz/dot_general | solution.py:31
  111.9 2.6 %fusion.9 = f32[8,256,256]{2,1,0:T(8,128)S(1)} fusion(f32[8,256,256]{2,1,0:T(8,128)S(1)} %fusion.27, f32[256]{0:T(256)S(1)} %fusion.37, s32[8]{0:T(128)S(1)} %fusion.36, s32[256,256]{0,1:T(8,128)S(1)} %broadcast_add_fusion), kind=kOutput, calls=%fused_computation.11 | convolution fusion | flops 810483712 | bytes 4457504 | tf_op jit(solution)/shard_map/ky,xyz->xkz/dot_general | solution.py:31
  114.5 2.7 %fusion.5 = f32[8,256,256]{2,1,0:T(8,128)S(1)} fusion(f32[8,256,256]{2,1,0:T(8,128)S(1)} %fusion.9), kind=kOutput, calls=%fused_computation.7 | convolution fusion | flops 806289408 | bytes 4194304 | tf_op jit(solution)/shard_map/kz,xyz->xyk/dot_general | solution.py:31
  117.2 2.1 %reshape.90 = f32[8,16,16,2,128]{4,3,2,1,0:T(2,128)} reshape(f32[8,256,256]{2,1,0:T(8,128)S(1)} %fusion.5) | data formatting | bytes 4194304 | tf_op jit(solution)/shard_map/reshape | solution.py:283
  119.3 3.2 %copy.13 = f32[8,16,16,2,128]{4,2,0,3,1:T(8,128)} copy(f32[8,16,16,2,128]{4,3,2,1,0:T(2,128)} %reshape.90) | data formatting | bytes 4194304 | tf_op jit(solution)/shard_map/reshape | solution.py:283
  122.5 0.0 copy-start.4
  122.5 0.0 copy-start.5
  122.5 5.3 %all-to-all-start.1 = ((f32[32,8,16,128]{3,2,1,0:T(8,128)}), f32[32,8,16,128]{3,2,1,0:T(8,128)S(1)}, u32[]{:S(2)}, u32[]{:S(2)}) async-start(f32[32,8,16,128]{3,2,1,0:T(8,128)} %bitcast.44), calls=%async_computation.1 | async-start | bytes 4194304 | tf_op jit(solution)/shard_map/all_to_all | solution.py:285
  127.8 0.0 copy-done.4
  127.8 0.0 copy-done.5
  127.8 0.1 pad_maximum_fusion.1
  127.9 1.5 collective-permute-start.5
  129.4 0.0 copy-done.7
  129.4 0.0 collective-permute-start.3
  129.4 0.0 copy-done.6
  129.4 2.6 %collective-permute-start.4 = (f32[2,128,256]{2,1,0:T(8,128)S(1)}, f32[2,128,256]{2,1,0:T(8,128)S(1)}, u32[]{:S(2)}, u32[]{:S(2)}) collective-permute-start(f32[2,128,256]{2,1,0:T(8,128)S(1)} %copy-done.6), channel_id=1, source_target_pairs={{2,0},{4,2},{6,4},{8,6},{10,8},{12,10},{14,12},{16,14},{18,16},{20... | collective-permute-start | bytes 786440 | tf_op jit(solution)/shard_map/ppermute | solution.py:202
  132.1 13.0 %collective-permute-done.5 = f32[2,2,16,1,256]{4,3,2,1,0:T(1,128)S(1)} collective-permute-done((f32[2,2,16,1,256]{4,3,2,1,0:T(1,128)S(1)}, f32[2,2,16,1,256]{4,3,2,1,0:T(1,128)S(1)}, u32[]{:S(2)}, u32[]{:S(2)}) %collective-permute-start.5) | collective-permute-done | bytes 65568 | tf_op jit(solution)/shard_map/ppermute | solution.py:199
  145.0 0.6 slice_bitcast_fusion.2
  145.7 32.4 %collective-permute-done.3.y_low_ref = f32[2,128,256]{2,1,0:T(8,128)S(1)} collective-permute-done((f32[2,128,256]{2,1,0:T(8,128)S(1)}, f32[2,128,256]{2,1,0:T(8,128)S(1)}, u32[]{:S(2)}, u32[]{:S(2)}) %collective-permute-start.3) | collective-permute-done | bytes 262176 | tf_op jit(solution)/shard_map/ppermute | solution.py:202
  178.1 0.0 collective-permute-done.4.y_high_ref
  178.1 0.7 copy-done.2
  178.8 0.1 copy-done.3
  178.9 5.9 %shard_map.71 = f32[2,16,128,256]{3,2,1,0:T(8,128)} custom-call(f32[2,16,128,256]{3,2,1,0:T(8,128)} %get-tuple-element.20.w_ref.w_prev.w_next, f32[2,16,128,256]{3,2,1,0:T(8,128)} %get-tuple-element.20.w_ref.w_prev.w_next, f32[2,16,128,256]{3,2,1,0:T(8,128)} %get-tuple-element.20.w_ref.w_prev.w_next, f32[2,128,256]{2,1,0:T(8,128)} %copy-done.2, ...), custom_call_target="tpu_custom_call" | custom-call | tf_op jit(solution)/shard_map/pallas_call | solution.py:245
  184.9 0.0 all-to-all-done.1
  184.9 4.3 %fusion.11 = f32[16,128,256]{2,1,0:T(8,128)} fusion(f32[256,16,128]{2,1,0:T(8,128)S(1)} %bitcast.43), kind=kOutput, calls=%fused_computation.12 | convolution fusion | flops 806813696 | bytes 4194304 | tf_op jit(solution)/shard_map/kn,nyz->yzk/dot_general | solution.py:31
  (7 shorter events, 0.0 us)
Async XLA Ops:
  6.1 19.3 %collective-permute-start = (f32[6,128,256]{2,1,0:T(8,128)}, f32[6,128,256]{2,1,0:T(8,128)S(1)}, u32[]{:S(2)}, u32[]{:S(2)}) collective-permute-start(f32[6,128,256]{2,1,0:T(8,128)} %get-tuple-element.16), channel_id=1, source_target_pairs={{0,2},{2,4},{4,6},{6,8},{8,10},{10,12},{12,14},{14,16},{16,18},{18... | collective-permute-start | bytes 2359304 | tf_op jit(solution)/shard_map/ppermute | solution.py:202
  6.2 19.2 %collective-permute-start.1 = (f32[6,128,256]{2,1,0:T(8,128)}, f32[6,128,256]{2,1,0:T(8,128)S(1)}, u32[]{:S(2)}, u32[]{:S(2)}) collective-permute-start(f32[6,128,256]{2,1,0:T(8,128)} %get-tuple-element.17), channel_id=1, source_target_pairs={{2,0},{4,2},{6,4},{8,6},{10,8},{12,10},{14,12},{16,14},{18,16},{20... | collective-permute-start | bytes 2359304 | tf_op jit(solution)/shard_map/ppermute | solution.py:202
  10.0 14.6 %collective-permute-start.2 = (f32[2,6,16,1,256]{4,3,2,1,0:T(1,128)S(1)}, f32[2,6,16,1,256]{4,3,2,1,0:T(1,128)S(1)}, u32[]{:S(2)}, u32[]{:S(2)}) collective-permute-start(f32[2,6,16,1,256]{4,3,2,1,0:T(1,128)S(1)} %pad_maximum_fusion), channel_id=1, source_target_pairs={{0,1},{1,0},{2,3},{3,2},{4,5},{5,4},{6,7},{7,6},{8,9},{9,8},{10,11... | collective-permute-start | bytes 589832 | tf_op jit(solution)/shard_map/ppermute | solution.py:199
  25.4 1.0 copy-start
  25.4 1.2 copy-start.1
  47.8 53.9 %all-to-all-start = ((f32[32,8,16,128]{3,2,1,0:T(8,128)}), f32[32,8,16,128]{3,2,1,0:T(8,128)S(1)}, u32[]{:S(2)}, u32[]{:S(2)}) async-start(f32[32,8,16,128]{3,2,1,0:T(8,128)} %copy.9), calls=%async_computation | async-start | bytes 4194304 | tf_op jit(solution)/shard_map/all_to_all | solution.py:270
  122.5 5.3 %copy-start.4 = (f32[2,16,1,256]{3,2,1,0:T(1,128)S(1)}, f32[2,16,1,256]{3,2,1,0:T(1,128)}, u32[]{:S(2)}) copy-start(f32[2,16,1,256]{3,2,1,0:T(1,128)} %get-tuple-element.24) | copy-start | bytes 98308
  122.5 5.3 %copy-start.5 = (f32[2,16,1,256]{3,2,1,0:T(1,128)S(1)}, f32[2,16,1,256]{3,2,1,0:T(1,128)}, u32[]{:S(2)}) copy-start(f32[2,16,1,256]{3,2,1,0:T(1,128)} %get-tuple-element.23) | copy-start | bytes 98308
  122.5 6.9 %copy-start.7 = (f32[2,128,256]{2,1,0:T(8,128)S(1)}, f32[2,128,256]{2,1,0:T(8,128)}, u32[]{:S(2)}) copy-start(f32[2,128,256]{2,1,0:T(8,128)} %get-tuple-element.21) | copy-start | bytes 786436
  122.5 6.9 %copy-start.6 = (f32[2,128,256]{2,1,0:T(8,128)S(1)}, f32[2,128,256]{2,1,0:T(8,128)}, u32[]{:S(2)}) copy-start(f32[2,128,256]{2,1,0:T(8,128)} %get-tuple-element.22) | copy-start | bytes 786436
  122.5 62.4 %all-to-all-start.1 = ((f32[32,8,16,128]{3,2,1,0:T(8,128)}), f32[32,8,16,128]{3,2,1,0:T(8,128)S(1)}, u32[]{:S(2)}, u32[]{:S(2)}) async-start(f32[32,8,16,128]{3,2,1,0:T(8,128)} %bitcast.44), calls=%async_computation.1 | async-start | bytes 4194304 | tf_op jit(solution)/shard_map/all_to_all | solution.py:285
  127.9 17.2 %collective-permute-start.5 = (f32[2,2,16,1,256]{4,3,2,1,0:T(1,128)S(1)}, f32[2,2,16,1,256]{4,3,2,1,0:T(1,128)S(1)}, u32[]{:S(2)}, u32[]{:S(2)}) collective-permute-start(f32[2,2,16,1,256]{4,3,2,1,0:T(1,128)S(1)} %pad_maximum_fusion.1), channel_id=1, source_target_pairs={{0,1},{1,0},{2,3},{3,2},{4,5},{5,4},{6,7},{7,6},{8,9},{9,8},{10,11... | collective-permute-start | bytes 196616 | tf_op jit(solution)/shard_map/ppermute | solution.py:199
  129.4 48.7 %collective-permute-start.3 = (f32[2,128,256]{2,1,0:T(8,128)S(1)}, f32[2,128,256]{2,1,0:T(8,128)S(1)}, u32[]{:S(2)}, u32[]{:S(2)}) collective-permute-start(f32[2,128,256]{2,1,0:T(8,128)S(1)} %copy-done.7), channel_id=1, source_target_pairs={{0,2},{2,4},{4,6},{6,8},{8,10},{10,12},{12,14},{14,16},{16,18},{18... | collective-permute-start | bytes 786440 | tf_op jit(solution)/shard_map/ppermute | solution.py:202
  129.4 48.7 %collective-permute-start.4 = (f32[2,128,256]{2,1,0:T(8,128)S(1)}, f32[2,128,256]{2,1,0:T(8,128)S(1)}, u32[]{:S(2)}, u32[]{:S(2)}) collective-permute-start(f32[2,128,256]{2,1,0:T(8,128)S(1)} %copy-done.6), channel_id=1, source_target_pairs={{2,0},{4,2},{6,4},{8,6},{10,8},{12,10},{14,12},{16,14},{18,16},{20... | collective-permute-start | bytes 786440 | tf_op jit(solution)/shard_map/ppermute | solution.py:202
  178.1 0.7 copy-start.2
  178.1 0.8 copy-start.3
